TPU v7x, 32 devices: a whole 2x2x4 slice. The times are simulated.
32 devices in a mesh: dom: 8 (over y, x, core), dest: 4 (over z).
Axes of the slice: x: 2, y: 2, z: 4, core: 2. Of those that a mesh axis runs over, the one named last changes fastest.
Arguments:
- cost: float32 [8192], P('dom'), may hold values from 0.2 to 1.5
- turn_weight: float32 [128, 64, 512], P('dom'), may hold values from 0.0005859375 to 0.01171875
- exit_value: float32 [192, 8192], P('dest', 'dom'), may hold values from 0.05 to 1
- demand: float32 [192, 8192], P('dest', 'dom'), may hold values from 0.02 to 1
- dest_weight: float32 [192], P('dest'), may hold values from 0.3 to 3
- slot_count: int32 [128], P('dom'), may hold values from 1 to 8
- col_ref: int32 [128, 8], P('dom'), may hold values from 0 to 31, as said below
- send_blocks: int32 [8, 8, 2], replicated, may hold values from 0 to 15
Outputs:
- flows: float32 [8192], P(('dom', 'dest'))
- cost_grad: float32 [8192], P(('dom', 'dest'))
Inputs may be any that keep to these rules, and one draw needn't show every extreme that they name: `col_ref`: A value below 16 names a block of the row block's own partition; a value 16 + p * 2 + c names block send_blocks[p, o, c] of partition p, o being the row block's partition.
All inputs are finite; a program needn't handle non-finite values.
Results may differ from a plain program's by a relative error of at most 0.0001.
Values sent between devices are 32-bit elements; how exact they have to be, the bound alone decides.
No kernel may reach another device: no remote copies, remote signals or barrier semaphores. Data moves between devices by JAX's collectives and lax.ppermute only.
A program may use at most 128 MiB of HBM per device.

v0:
```python
import jax
import jax.numpy as jnp
from jax import lax
from jax.sharding import PartitionSpec as P


def local(cost, turn_weight, exit_value, demand, dest_weight, slot_count, col_ref, send_blocks):
    blocks = col_ref.shape[0]
    slot_total = col_ref.shape[1]
    block_len = turn_weight.shape[1]
    columns = exit_value.shape[0]
    capacity = send_blocks.shape[2]
    partitions = lax.axis_size("dom")
    my_part = lax.axis_index("dom")
    live_slots = (jnp.arange(slot_total, dtype=jnp.int32)[None, :] < slot_count[:, None]).astype(
        jnp.float32
    )
    turn_matrix = (
        turn_weight.reshape(blocks, block_len, slot_total, block_len) * live_slots[:, None, :, None]
    )
    link_scale = jnp.exp(-cost)
    outbound = lax.dynamic_index_in_dim(send_blocks, my_part, 0, keepdims=False)
    value = exit_value
    for sweep in range(2):
        weighted = (value * link_scale[None, :]).reshape(columns, blocks, block_len)
        forward_outgoing = weighted[:, outbound.reshape(-1), :].reshape(
            columns, partitions, capacity * block_len
        )
        received = lax.all_to_all(forward_outgoing, "dom", split_axis=1, concat_axis=1, tiled=True)
        table = jnp.concatenate(
            [weighted, received.reshape(columns, partitions * capacity, block_len)], axis=1
        )
        picked = table[:, col_ref, :]
        result = jnp.einsum("dnsj,nisj->dni", picked, turn_matrix, precision=lax.Precision.HIGHEST)
        value = result.reshape(columns, blocks * block_len) + exit_value
    load = demand
    back = demand
    for sweep in range(2):
        ratio = load / value
        shaped = ratio.reshape(columns, blocks, block_len)
        terms = jnp.einsum("dni,nisj->dnsj", shaped, turn_matrix, precision=lax.Precision.HIGHEST)
        totals = (
            jnp.zeros((columns, blocks + partitions * capacity, block_len), jnp.float32)
            .at[:, col_ref, :]
            .add(terms)
        )
        outgoing = totals[:, blocks:, :].reshape(columns, partitions, capacity * block_len)
        returned = lax.all_to_all(outgoing, "dom", split_axis=1, concat_axis=1, tiled=True)
        owned = (
            totals[:, :blocks, :]
            .at[:, outbound.reshape(-1), :]
            .add(returned.reshape(columns, partitions * capacity, block_len))
        )
        back = owned.reshape(columns, blocks * block_len) * link_scale[None, :]
        load = value * back + demand
    dest_total = columns * lax.axis_size("dest")
    flow_part = jnp.sum(load, axis=0) / dest_total
    grad_part = -jnp.sum(dest_weight[:, None] * value * back, axis=0) / dest_total
    flow_all, grad_all = lax.psum((flow_part, grad_part), "dest")
    share = flow_part.shape[0] // lax.axis_size("dest")
    start = lax.axis_index("dest") * share
    flows = lax.dynamic_slice_in_dim(flow_all, start, share)
    cost_grad = lax.dynamic_slice_in_dim(grad_all, start, share)
    return (flows, cost_grad)


def solution(mesh):
    placed = (
        P("dom"),
        P("dom", None, None),
        P("dest", "dom"),
        P("dest", "dom"),
        P("dest"),
        P("dom"),
        P("dom", None),
        P(),
    )
    return jax.shard_map(
        local,
        mesh=mesh,
        in_specs=placed,
        out_specs=(P(("dom", "dest")), P(("dom", "dest"))),
        check_vma=False,
    )
```

profile of v0, /device:TPU:0, one launch (start us, length us, event | category | flops | bytes accessed | tf_op | source)
XLA Modules:
  0.0 126.2 jit_solution(4871890688594458419)
XLA Ops:
  0.7 0.7 copy-done
  1.5 0.7 negate_exponential_fusion
  2.2 0.9 broadcast_multiply_fusion
  3.4 0.6 gather_fusion
  4.0 0.1 copy.54
  4.3 0.7 copy.55
  5.0 5.2 %all-to-all-start = ((f32[48,8,128]{2,0,1:T(8,128)}), f32[48,8,128]{2,0,1:T(8,128)S(1)}, u32[]{:S(2)}, u32[]{:S(2)}) async-start(f32[48,8,128]{2,0,1:T(8,128)} %copy.55), calls=%async_computation | async-start | bytes 393216 | tf_op jit(solution)/shard_map/all_to_all | solution.py:29
  10.4 2.4 %reshape.113 = f32[16,64,8,64]{3,2,1,0:T(8,128)} reshape(f32[16,64,512]{2,1,0:T(8,128)S(1)} %copy-done.1) | data formatting | bytes 4194304 | tf_op jit(solution)/shard_map/reshape | solution.py:19
  12.8 3.6 %all-to-all-done = f32[48,8,128]{2,0,1:T(8,128)S(1)} async-done(((f32[48,8,128]{2,0,1:T(8,128)}), f32[48,8,128]{2,0,1:T(8,128)S(1)}, u32[]{:S(2)}, u32[]{:S(2)}) %all-to-all-start) | async-done | bytes 196640 | tf_op jit(solution)/shard_map/all_to_all | solution.py:29
  16.8 2.5 %gather_fusion.1 = f32[128,48,64]{2,1,0:T(8,128)} fusion(f32[48,32,64]{2,0,1:T(8,128)S(1)} %pad_maximum_fusion, s32[1024]{0:T(1024)S(1)} %pad_clamp_fusion), kind=kCustom, calls=%fused_computation.1 | custom fusion | bytes 3146240 | tf_op jit(solution)/shard_map/gather | solution.py:33
  19.3 7.8 %fusion.8 = f32[48,16,64]{2,0,1:T(8,128)S(1)} fusion(f32[48,16,8,64]{3,0,2,1:T(8,128)} %bitcast.35, f32[16,64,8,64]{3,2,1,0:T(8,128)} %reshape.113, f32[16,8]{1,0:T(8,128)S(1)} %fusion.12), kind=kOutput, calls=%fused_computation.17 | convolution fusion | flops 302514176 | bytes 3867136 | tf_op jit(solution)/shard_map/dnsj,nisj->dni/dot_general | solution.py:34
  27.2 0.2 reshape.118
  27.7 0.6 gather_fusion.2
  28.5 8.6 %all_to_all.20 = f32[48,8,128]{2,0,1:T(8,128)S(1)} all-to-all(f32[48,8,128]{2,0,1:T(8,128)S(1)} %copy.63), channel_id=1, replica_groups=mesh['dom'=8,'dest'=4] {'dom'}, dimensions={1} | all-to-all | bytes 393216 | tf_op jit(solution)/shard_map/all_to_all | solution.py:29
  37.6 2.5 %gather_fusion.3 = f32[128,48,64]{2,1,0:T(8,128)} fusion(f32[48,32,64]{2,0,1:T(8,128)S(1)} %pad_maximum_fusion.1, s32[1024]{0:T(1024)S(1)} %pad_clamp_fusion), kind=kCustom, calls=%fused_computation.3 | custom fusion | bytes 3146240 | tf_op jit(solution)/shard_map/gather | solution.py:33
  40.0 7.8 %fusion.9 = f32[48,16,64]{2,0,1:T(8,128)S(1)} fusion(f32[48,16,8,64]{3,0,2,1:T(8,128)} %bitcast.34, f32[16,64,8,64]{3,2,1,0:T(8,128)} %reshape.113, f32[16,8]{1,0:T(8,128)S(1)} %fusion.12), kind=kOutput, calls=%fused_computation.18 | convolution fusion | flops 302514176 | bytes 3867136 | tf_op jit(solution)/shard_map/dnsj,nisj->dni/dot_general | solution.py:34
  48.0 0.2 reshape.122
  48.3 7.5 %fusion.1 = f32[16,8,64,48]{2,3,1,0:T(8,128)} fusion(f32[16,64,8,64]{3,2,1,0:T(8,128)} %reshape.113, f32[16,8]{1,0:T(8,128)S(1)} %fusion.12, f32[48,16,64,1]{2,1,0,3:T(8,128)S(1)} %bitcast.37), kind=kOutput, calls=%fused_computation.10 | convolution fusion | flops 302514176 | bytes 3867136 | tf_op jit(solution)/shard_map/dni,nisj->dnsj/dot_general | solution.py:41
  55.8 12.7 %scatter_fusion = f32[48,32,64]{2,0,1:T(8,128)S(1)} fusion(f32[48,32,64]{2,0,1:T(8,128)S(1)} %broadcast.53.clone, s32[128]{0:T(128)S(1)} %reshape.141, f32[128,48,64]{2,1,0:T(8,128)} %bitcast.33), kind=kCustom, calls=%fused_computation.4 | custom fusion | flops 393216 | bytes 4719104 | tf_op jit(solution)/shard_map/scatter-add | solution.py:45
  68.9 8.6 %all_to_all.21 = f32[48,8,128]{2,0,1:T(8,128)S(1)} all-to-all(f32[48,8,128]{2,0,1:T(8,128)S(1)} %copy.70), channel_id=1, replica_groups=mesh['dom'=8,'dest'=4] {'dom'}, dimensions={1} | all-to-all | bytes 393216 | tf_op jit(solution)/shard_map/all_to_all | solution.py:48
  77.8 1.4 %scatter_fusion.1 = f32[48,16,64]{2,0,1:T(8,128)S(1)} fusion(f32[48,16,64]{2,0,1:T(8,128)S(1)} %get-tuple-element.11, s32[16]{0:T(128)S(1)} %fusion.13, f32[16,48,64]{2,1,0:T(8,128)S(1)} %copy.72), kind=kCustom, calls=%fused_computation.5 | custom fusion | flops 49152 | bytes 589888 | tf_op jit(solution)/shard_map/scatter-add | solution.py:52
  79.4 0.2 reshape.126
  79.8 7.5 %fusion = f32[16,8,64,48]{2,3,1,0:T(8,128)} fusion(f32[16,64,8,64]{3,2,1,0:T(8,128)} %reshape.113, f32[16,8]{1,0:T(8,128)S(1)} %fusion.12, f32[48,16,64,1]{2,1,0,3:T(8,128)S(1)} %bitcast.36), kind=kOutput, calls=%fused_computation.9 | convolution fusion | flops 302514176 | bytes 3867136 | tf_op jit(solution)/shard_map/dni,nisj->dnsj/dot_general | solution.py:41
  87.3 12.7 %scatter_fusion.2 = f32[48,32,64]{2,0,1:T(8,128)S(1)} fusion(f32[48,32,64]{2,0,1:T(8,128)S(1)} %broadcast.53, s32[128]{0:T(128)S(1)} %reshape.141, f32[128,48,64]{2,1,0:T(8,128)} %bitcast.32), kind=kCustom, calls=%fused_computation.6 | custom fusion | flops 393216 | bytes 4719104 | tf_op jit(solution)/shard_map/scatter-add | solution.py:45
  100.3 0.7 copy.76
  101.0 3.4 %all-to-all-start.3 = ((f32[48,8,128]{2,0,1:T(8,128)}), f32[48,8,128]{2,0,1:T(8,128)S(1)}, u32[]{:S(2)}, u32[]{:S(2)}) async-start(f32[48,8,128]{2,0,1:T(8,128)} %copy.76), calls=%async_computation.3 | async-start | bytes 393216 | tf_op jit(solution)/shard_map/all_to_all | solution.py:48
  104.4 6.1 %all-to-all-done.3 = f32[48,8,128]{2,0,1:T(8,128)S(1)} async-done(((f32[48,8,128]{2,0,1:T(8,128)}), f32[48,8,128]{2,0,1:T(8,128)S(1)}, u32[]{:S(2)}, u32[]{:S(2)}) %all-to-all-start.3) | async-done | bytes 196640 | tf_op jit(solution)/shard_map/all_to_all | solution.py:48
  110.9 1.4 %scatter_fusion.3 = f32[48,16,64]{2,0,1:T(8,128)S(1)} fusion(f32[48,16,64]{2,0,1:T(8,128)S(1)} %get-tuple-element.9, s32[16]{0:T(128)S(1)} %fusion.13, f32[16,48,64]{2,1,0:T(8,128)S(1)} %copy.78), kind=kCustom, calls=%fused_computation.7 | custom fusion | flops 49152 | bytes 589888 | tf_op jit(solution)/shard_map/scatter-add | solution.py:52
  112.5 0.2 reshape.130
  112.8 12.1 %all-reduce = (f32[1024]{0:T(1024)S(1)}, f32[1024]{0:T(1024)S(1)}) all-reduce(f32[1024]{0:T(1024)S(1)} %get-tuple-element.13, f32[1024]{0:T(1024)S(1)} %get-tuple-element.12), channel_id=1, replica_groups=mesh['dom'=8,'dest'=4] {'dest'}, use_global_device_ids=true, to_apply=%region_5.6 | all-reduce | flops 2048 | bytes 16384 | tf_op jit(solution)/shard_map/psum | solution.py:59
  124.9 0.6 dynamic_slice.12
  125.5 0.6 dynamic_slice.11
  (65 shorter events, 4.4 us)
Async XLA Ops:
  0.6 0.7 copy-start
  0.6 9.5 %copy-start.4 = (s32[16,8]{0,1:T(8,128)S(1)}, s32[16,8]{0,1:T(8,128)}, u32[]{:S(2)}) copy-start(s32[16,8]{0,1:T(8,128)} %param.14) | copy-start | bytes 1540
  0.7 9.7 %copy-start.1 = (f32[16,64,512]{2,1,0:T(8,128)S(1)}, f32[16,64,512]{2,1,0:T(8,128)}, u32[]{:S(2)}) copy-start(f32[16,64,512]{2,1,0:T(8,128)} %param.9) | copy-start | bytes 6291460
  4.0 8.7 %copy-start.5 = (s32[16]{0:T(128)S(1)}, s32[16]{0:T(128)}, u32[]{:S(2)}) copy-start(s32[16]{0:T(128)} %param.13) | copy-start | bytes 196
  5.0 11.4 %all-to-all-start = ((f32[48,8,128]{2,0,1:T(8,128)}), f32[48,8,128]{2,0,1:T(8,128)S(1)}, u32[]{:S(2)}, u32[]{:S(2)}) async-start(f32[48,8,128]{2,0,1:T(8,128)} %copy.55), calls=%async_computation | async-start | bytes 393216 | tf_op jit(solution)/shard_map/all_to_all | solution.py:29
  19.3 8.1 %copy-start.2 = (f32[48,1024]{1,0:T(8,128)S(1)}, f32[48,1024]{1,0:T(8,128)}, u32[]{:S(2)}) copy-start(f32[48,1024]{1,0:T(8,128)} %param.10) | copy-start | bytes 589828
  40.0 8.1 %copy-start.3 = (f32[48,1024]{1,0:T(8,128)S(1)}, f32[48,1024]{1,0:T(8,128)}, u32[]{:S(2)}) copy-start(f32[48,1024]{1,0:T(8,128)} %param.11) | copy-start | bytes 589828
  100.0 12.7 %copy-start.6 = (f32[48]{0:T(128)S(1)}, f32[48]{0:T(128)}, u32[]{:S(2)}) copy-start(f32[48]{0:T(128)} %param.12) | copy-start | bytes 580
  101.0 9.5 %all-to-all-start.3 = ((f32[48,8,128]{2,0,1:T(8,128)}), f32[48,8,128]{2,0,1:T(8,128)S(1)}, u32[]{:S(2)}, u32[]{:S(2)}) async-start(f32[48,8,128]{2,0,1:T(8,128)} %copy.76), calls=%async_computation.3 | async-start | bytes 393216 | tf_op jit(solution)/shard_map/all_to_all | solution.py:48
where the time goes:
time: 127 us; the launch traced here: 126 us
  matrix products  30.5 us (24%)
  other arithmetic  30.4 us (24%)
  blocking collectives  29.3 us (23%)
  local copies, waits for them, and re-layouts  16.6 us (13%)
  waiting for transfers between devices  9.69 us (8%)
  starting transfers between devices  8.59 us (7%)
    scatter-add x2, other arithmetic, local(): totals = jnp.zeros((columns, blocks + partitions * capacity, block_len),...  25.4 us
    dot_general x2, matrix products, local(): jnp.einsum('dnsj,nisj->dni', picked, turn_matrix, precision=lax.Precision...  15.6 us
    dot_general x2, matrix products, local(): jnp.einsum('dni,nisj->dnsj', shaped, turn_matrix, precision=lax.Precision...  14.9 us
    psum x1, blocking collectives, local(): flow_all, grad_all = lax.psum((flow_part, grad_part), 'dest')  12.1 us
    all_to_all x1, blocking collectives, local(): lax.all_to_all(forward_outgoing, 'dom', split_axis=1, concat_axis=1, tile...  8.6 us
    all_to_all x1, blocking collectives, local(): lax.all_to_all(outgoing, 'dom', split_axis=1, concat_axis=1, tiled=True)  8.6 us
    all_to_all x1, waiting for transfers between devices, local(): lax.all_to_all(outgoing, 'dom', split_axis=1, concat_axis=1, tiled=True)  6.13 us
    all_to_all x1, starting transfers between devices, local(): lax.all_to_all(forward_outgoing, 'dom', split_axis=1, concat_axis=1, tile...  5.2 us
  transfers between devices with their start and end apart: 2, of which 2 were waited for; matrix products, arithmetic and copies ran while one was open for 2% of the time, Pallas kernels for 0%

commit v1 on v0

v1 whole, which is shorter than its diff:
```python
import jax
import jax.numpy as jnp
from jax import lax
from jax.sharding import PartitionSpec as P

USE_PERMUTES = False
ONEHOT_SCATTER = True


def shift_pairs(count, shift):
    return [(j, (j + shift) % count) for j in range(count)]


def local(cost, turn_weight, exit_value, demand, dest_weight, slot_count, col_ref, send_blocks):
    blocks = col_ref.shape[0]
    slot_total = col_ref.shape[1]
    block_len = turn_weight.shape[1]
    columns = exit_value.shape[0]
    capacity = send_blocks.shape[2]
    partitions = lax.axis_size("dom")
    my_part = lax.axis_index("dom")
    table_blocks = blocks + partitions * capacity
    live = jnp.arange(slot_total, dtype=jnp.int32)[None, :] < slot_count[:, None]
    turn_matrix = turn_weight.reshape(blocks, block_len, slot_total, block_len) * live[
        :, None, :, None
    ].astype(jnp.float32)
    link_scale = jnp.exp(-cost)
    if USE_PERMUTES:
        ghost = jnp.maximum(col_ref - blocks, 0)
        source = ghost // capacity
        slot_of = blocks + ((my_part - source) % partitions) * capacity + ghost % capacity
        col_idx = jnp.where(col_ref < blocks, col_ref, slot_of)
        peers = (my_part + jnp.arange(partitions, dtype=jnp.int32)) % partitions
        outbound = send_blocks[my_part][peers].reshape(-1)
    else:
        col_idx = col_ref
        outbound = lax.dynamic_index_in_dim(send_blocks, my_part, 0, keepdims=False).reshape(-1)
    onehot = (
        (col_idx[:, :, None] == jnp.arange(table_blocks, dtype=jnp.int32)[None, None, :])
        & live[:, :, None]
    ).astype(jnp.float32)

    def exchange(pieces, sign):
        if not USE_PERMUTES:
            return lax.all_to_all(pieces, "dom", split_axis=1, concat_axis=1, tiled=True)
        got = [pieces[:, 0]]
        for s in range(1, partitions):
            got.append(lax.ppermute(pieces[:, s], "dom", shift_pairs(partitions, sign * s)))
        return jnp.stack(got, axis=1)

    value = exit_value
    for sweep in range(2):
        weighted = value * link_scale[None, :]
        shaped = weighted.reshape(columns, blocks, block_len)
        forward_outgoing = shaped[:, outbound, :].reshape(columns, partitions, capacity * block_len)
        received = exchange(forward_outgoing, 1)
        table = jnp.concatenate(
            [shaped, received.reshape(columns, partitions * capacity, block_len)], axis=1
        )
        picked = table[:, col_idx, :]
        result = jnp.einsum("dnsj,nisj->dni", picked, turn_matrix, precision=lax.Precision.HIGH)
        value = result.reshape(columns, blocks * block_len) + exit_value
    load = demand
    back = demand
    for sweep in range(2):
        ratio = load / value
        shaped = ratio.reshape(columns, blocks, block_len)
        terms = jnp.einsum("dni,nisj->dnsj", shaped, turn_matrix, precision=lax.Precision.HIGH)
        if ONEHOT_SCATTER:
            totals = jnp.einsum("dnsj,nsb->dbj", terms, onehot, precision=lax.Precision.HIGHEST)
        else:
            totals = (
                jnp.zeros((columns, table_blocks, block_len), jnp.float32)
                .at[:, col_idx, :]
                .add(terms)
            )
        outgoing = totals[:, blocks:, :].reshape(columns, partitions, capacity * block_len)
        returned = exchange(outgoing, -1)
        owned = (
            totals[:, :blocks, :]
            .at[:, outbound, :]
            .add(returned.reshape(columns, partitions * capacity, block_len))
        )
        back = owned.reshape(columns, blocks * block_len) * link_scale[None, :]
        load = value * back + demand
    dest_total = columns * lax.axis_size("dest")
    flow_part = jnp.sum(load, axis=0) / dest_total
    grad_part = -jnp.sum(dest_weight[:, None] * value * back, axis=0) / dest_total
    stacked = jnp.stack([flow_part, grad_part], axis=1)
    dest_n = lax.axis_size("dest")
    me = lax.axis_index("dest")
    parts = stacked.reshape(dest_n, -1, 2)
    both = lax.dynamic_index_in_dim(parts, me, 0, keepdims=False)
    for shift in range(1, dest_n):
        send = lax.dynamic_index_in_dim(parts, (me + shift) % dest_n, 0, keepdims=False)
        both = both + lax.ppermute(send, "dest", shift_pairs(dest_n, shift))
    return (both[:, 0], both[:, 1])


def solution(mesh):
    placed = (
        P("dom"),
        P("dom", None, None),
        P("dest", "dom"),
        P("dest", "dom"),
        P("dest"),
        P("dom"),
        P("dom", None),
        P(),
    )
    return jax.shard_map(
        local,
        mesh=mesh,
        in_specs=placed,
        out_specs=(P(("dom", "dest")), P(("dom", "dest"))),
        check_vma=False,
    )
```

time: 127 us -> 95.4 us (0.75)
  other arithmetic: 30.4 us -> 5.73 us
  blocking collectives: 29.3 us -> 8.6 us
  waiting for transfers between devices: 9.69 us -> 19.8 us
  starting transfers between devices: 8.59 us -> 16.9 us
  matrix products: 30.5 us -> 26.7 us
    scatter-add x4 -> x2, other arithmetic: 28.3 us -> 2.89 us  [local(): owned = totals[:, :blocks, :].at[:, outbound, :].add(returned.reshape(col...]
    psum x1 -> x0, blocking collectives: 12.1 us -> none  [local(): flow_all, grad_all = lax.psum((flow_part, grad_part), 'dest')]
    all_to_all x2 -> x1, blocking collectives: 17.2 us -> 8.6 us  [exchange(): lax.all_to_all(pieces, 'dom', split_axis=1, concat_axis=1, tiled=True)]
    dot_general x2, matrix products: 14.9 us -> 8.78 us  [local(): jnp.einsum('dni,nisj->dnsj', shaped, turn_matrix, precision=lax.Precision...]
    dot_general x0 -> x2, matrix products: none -> 6.04 us  [local(): jnp.einsum('dnsj,nsb->dbj', terms, onehot, precision=lax.Precision.HIGHEST)]
    all_to_all x2 -> x3, waiting for transfers between devices: 9.69 us -> 15.4 us  [exchange(): lax.all_to_all(pieces, 'dom', split_axis=1, concat_axis=1, tiled=True)]
    ppermute x0 -> x3, starting transfers between devices: none -> 4.67 us  [local(): both = both + lax.ppermute(send, 'dest', shift_pairs(dest_n, shift))]
    ppermute x0 -> x3, waiting for transfers between devices: none -> 4.37 us  [local(): both = both + lax.ppermute(send, 'dest', shift_pairs(dest_n, shift))]
  transfers between devices with their start and end apart: 2 -> 6, of which waited for: 2 -> 6; matrix products, arithmetic and copies ran while one was open for 2% -> 3% of each run, Pallas kernels for 0% -> 0%
where the time goes in v1:
time: 95.4 us; the launch traced here: 94.9 us
  matrix products  26.7 us (28%)
  waiting for transfers between devices  19.8 us (21%)
  starting transfers between devices  16.9 us (18%)
  local copies, waits for them, and re-layouts  16 us (17%)
  blocking collectives  8.6 us (9%)
  other arithmetic  5.73 us (6%)
  between operations  1.18 us (1%)
    all_to_all x3, waiting for transfers between devices, exchange(): lax.all_to_all(pieces, 'dom', split_axis=1, concat_axis=1, tiled=True)  15.4 us
    all_to_all x3, starting transfers between devices, exchange(): lax.all_to_all(pieces, 'dom', split_axis=1, concat_axis=1, tiled=True)  12.2 us
    dot_general x2, matrix products, local(): jnp.einsum('dnsj,nisj->dni', picked, turn_matrix, precision=lax.Precision...  11.9 us
    dot_general x2, matrix products, local(): jnp.einsum('dni,nisj->dnsj', shaped, turn_matrix, precision=lax.Precision...  8.78 us
    all_to_all x1, blocking collectives, exchange(): lax.all_to_all(pieces, 'dom', split_axis=1, concat_axis=1, tiled=True)  8.6 us
    dot_general x2, matrix products, local(): jnp.einsum('dnsj,nsb->dbj', terms, onehot, precision=lax.Precision.HIGHEST)  6.04 us
    gather x2, local copies, waits for them, and re-layouts, local(): picked = table[:, col_idx, :]  4.98 us
    ppermute x3, starting transfers between devices, local(): both = both + lax.ppermute(send, 'dest', shift_pairs(dest_n, shift))  4.67 us
  transfers between devices with their start and end apart: 6, of which 6 were waited for; matrix products, arithmetic and copies ran while one was open for 3% of the time, Pallas kernels for 0%

profile of v1, /device:TPU:0, one launch (start us, length us, event | category | flops | bytes accessed | tf_op | source)
XLA Modules:
  0.0 94.9 jit_solution(17685159622169090147)
XLA Ops:
  0.7 0.8 negate_exponential_fusion
  1.5 0.9 %broadcast_multiply_fusion = f32[48,1024]{1,0:T(8,128)S(1)} fusion(f32[48,1024]{1,0:T(8,128)} %param.10, f32[1024]{0:T(1024)S(1)} %negate_exponential_fusion), kind=kLoop, calls=%fused_computation.33 | loop fusion | flops 49152 | bytes 397312 | tf_op jit(solution)/shard_map/mul | solution.py:53
  2.7 0.7 compare_select_fusion
  3.8 0.6 gather_fusion
  4.6 0.7 copy.59
  5.3 5.2 %all-to-all-start = ((f32[48,8,128]{2,0,1:T(8,128)}), f32[48,8,128]{2,0,1:T(8,128)S(1)}, u32[]{:S(2)}, u32[]{:S(2)}) async-start(f32[48,8,128]{2,0,1:T(8,128)} %copy.59), calls=%async_computation | async-start | bytes 393216 | tf_op jit(solution)/shard_map/all_to_all | solution.py:45
  10.5 2.4 %reshape.164 = f32[16,64,8,64]{3,2,1,0:T(8,128)} reshape(f32[16,64,512]{2,1,0:T(8,128)S(1)} %copy-done.1) | data formatting | bytes 4194304 | tf_op jit(solution)/shard_map/reshape | solution.py:24
  13.0 3.7 %all-to-all-done = f32[48,8,128]{2,0,1:T(8,128)S(1)} async-done(((f32[48,8,128]{2,0,1:T(8,128)}), f32[48,8,128]{2,0,1:T(8,128)S(1)}, u32[]{:S(2)}, u32[]{:S(2)}) %all-to-all-start) | async-done | bytes 196640 | tf_op jit(solution)/shard_map/all_to_all | solution.py:45
  17.1 2.5 %gather_fusion.1 = f32[128,48,64]{2,1,0:T(8,128)} fusion(f32[48,32,64]{2,0,1:T(8,128)S(1)} %pad_maximum_fusion, s32[1024]{0:T(1024)S(1)} %get-tuple-element.18), kind=kCustom, calls=%fused_computation.1 | custom fusion | bytes 3146240 | tf_op jit(solution)/shard_map/gather | solution.py:60
  19.6 5.9 %fusion.20 = f32[48,16,64]{2,0,1:T(8,128)S(1)} fusion(f32[48,16,8,64]{3,0,2,1:T(8,128)} %bitcast.62, f32[16,64,8,64]{3,2,1,0:T(8,128)} %reshape.164, f32[16,8]{1,0:T(8,128)S(1)} %copy.54), kind=kOutput, calls=%fused_computation.23 | convolution fusion | flops 151519232 | bytes 3867136 | tf_op jit(solution)/shard_map/dnsj,nisj->dni/dot_general | solution.py:61
  26.2 0.6 gather_fusion.2
  27.0 8.6 %all_to_all.20 = f32[48,8,128]{2,0,1:T(8,128)S(1)} all-to-all(f32[48,8,128]{2,0,1:T(8,128)S(1)} %copy.67), channel_id=1, replica_groups=mesh['dom'=8,'dest'=4] {'dom'}, dimensions={1} | all-to-all | bytes 393216 | tf_op jit(solution)/shard_map/all_to_all | solution.py:45
  36.0 2.5 %gather_fusion.3 = f32[128,48,64]{2,1,0:T(8,128)} fusion(f32[48,32,64]{2,0,1:T(8,128)S(1)} %pad_maximum_fusion.1, s32[1024]{0:T(1024)S(1)} %get-tuple-element.18), kind=kCustom, calls=%fused_computation.3 | custom fusion | bytes 3146240 | tf_op jit(solution)/shard_map/gather | solution.py:60
  38.5 5.9 %fusion.21 = f32[48,16,64]{2,0,1:T(8,128)S(1)} fusion(f32[48,16,8,64]{3,0,2,1:T(8,128)} %bitcast.61, f32[16,64,8,64]{3,2,1,0:T(8,128)} %reshape.164, f32[16,8]{1,0:T(8,128)S(1)} %copy.54), kind=kOutput, calls=%fused_computation.24 | convolution fusion | flops 151519232 | bytes 3867136 | tf_op jit(solution)/shard_map/dnsj,nisj->dni/dot_general | solution.py:61
  45.0 4.4 %fusion.12 = f32[48,16,8,64]{3,0,2,1:T(8,128)S(1)} fusion(f32[16,64,8,64]{3,2,1,0:T(8,128)} %reshape.164, f32[16,8]{1,0:T(8,128)S(1)} %copy.54, f32[48,16,64,1]{2,1,0,3:T(8,128)S(1)} %bitcast.64), kind=kOutput, calls=%fused_computation.19 | convolution fusion | flops 151519232 | bytes 3867136 | tf_op jit(solution)/shard_map/dni,nisj->dnsj/dot_general | solution.py:68
  49.4 3.0 %fusion.14 = f32[48,32,64]{2,1,0:T(8,128)S(1)} fusion(f32[48,16,8,64]{3,0,2,1:T(8,128)S(1)} %fusion.12, s32[16,8]{0,1:T(8,128)S(1)} %copy-done.4, pred[16,8]{0,1:T(8,128)(4,1)S(1)} %get-tuple-element.16), kind=kOutput, calls=%fused_computation.21 | convolution fusion | flops 151003136 | bytes 1966720 | tf_op jit(solution)/shard_map/dnsj,nsb->dbj/dot_general | solution.py:70
  52.6 0.7 copy.74
  53.3 3.6 %all-to-all-start.2 = ((f32[48,8,128]{2,0,1:T(8,128)}), f32[48,8,128]{2,0,1:T(8,128)S(1)}, u32[]{:S(2)}, u32[]{:S(2)}) async-start(f32[48,8,128]{2,0,1:T(8,128)} %copy.74), calls=%async_computation.2 | async-start | bytes 393216 | tf_op jit(solution)/shard_map/all_to_all | solution.py:45
  57.0 5.8 %all-to-all-done.2 = f32[48,8,128]{2,0,1:T(8,128)S(1)} async-done(((f32[48,8,128]{2,0,1:T(8,128)}), f32[48,8,128]{2,0,1:T(8,128)S(1)}, u32[]{:S(2)}, u32[]{:S(2)}) %all-to-all-start.2) | async-done | bytes 196640 | tf_op jit(solution)/shard_map/all_to_all | solution.py:45
  63.2 1.4 %scatter_fusion = f32[48,16,64]{2,0,1:T(8,128)S(1)} fusion(f32[48,16,64]{2,0,1:T(8,128)S(1)} %copy.76, s32[16]{0:T(128)S(1)} %fusion.34, f32[16,48,64]{2,1,0:T(8,128)S(1)} %copy.77), kind=kCustom, calls=%fused_computation.4 | custom fusion | flops 49152 | bytes 589888 | tf_op jit(solution)/shard_map/scatter-add | solution.py:82
  65.1 4.4 %fusion.13 = f32[48,16,8,64]{3,0,2,1:T(8,128)S(1)} fusion(f32[16,64,8,64]{3,2,1,0:T(8,128)} %reshape.164, f32[16,8]{1,0:T(8,128)S(1)} %copy.54, f32[48,16,64,1]{2,1,0,3:T(8,128)S(1)} %bitcast.63), kind=kOutput, calls=%fused_computation.20 | convolution fusion | flops 151519232 | bytes 3867136 | tf_op jit(solution)/shard_map/dni,nisj->dnsj/dot_general | solution.py:68
  69.5 3.0 %fusion.17 = f32[48,32,64]{2,1,0:T(8,128)S(1)} fusion(f32[48,16,8,64]{3,0,2,1:T(8,128)S(1)} %fusion.13, s32[16,8]{0,1:T(8,128)S(1)} %copy-done.4, pred[16,8]{0,1:T(8,128)(4,1)S(1)} %get-tuple-element.16), kind=kOutput, calls=%fused_computation.22 | convolution fusion | flops 151003136 | bytes 1966720 | tf_op jit(solution)/shard_map/dnsj,nsb->dbj/dot_general | solution.py:70
  72.7 0.7 copy.81
  73.4 3.4 %all-to-all-start.3 = ((f32[48,8,128]{2,0,1:T(8,128)}), f32[48,8,128]{2,0,1:T(8,128)S(1)}, u32[]{:S(2)}, u32[]{:S(2)}) async-start(f32[48,8,128]{2,0,1:T(8,128)} %copy.81), calls=%async_computation.3 | async-start | bytes 393216 | tf_op jit(solution)/shard_map/all_to_all | solution.py:45
  77.0 6.0 %all-to-all-done.3 = f32[48,8,128]{2,0,1:T(8,128)S(1)} async-done(((f32[48,8,128]{2,0,1:T(8,128)}), f32[48,8,128]{2,0,1:T(8,128)S(1)}, u32[]{:S(2)}, u32[]{:S(2)}) %all-to-all-start.3) | async-done | bytes 196640 | tf_op jit(solution)/shard_map/all_to_all | solution.py:45
  83.3 1.4 %scatter_fusion.1 = f32[48,16,64]{2,0,1:T(8,128)S(1)} fusion(f32[48,16,64]{2,0,1:T(8,128)S(1)} %copy.83, s32[16]{0:T(128)S(1)} %fusion.34, f32[16,48,64]{2,1,0:T(8,128)S(1)} %copy.84), kind=kCustom, calls=%fused_computation.5 | custom fusion | flops 49152 | bytes 589888 | tf_op jit(solution)/shard_map/scatter-add | solution.py:82
  85.2 3.7 %collective-permute-start.2 = (f32[256,2]{0,1:T(2,128)S(1)}, f32[256,2]{0,1:T(2,128)S(1)}, u32[]{:S(2)}, u32[]{:S(2)}) collective-permute-start(f32[256,2]{0,1:T(2,128)S(1)} %bitcast.69), channel_id=1, source_target_pairs={{0,3},{1,0},{2,1},{3,2},{4,7},{5,4},{6,5},{7,6},{8,11},{9,8},{10,9... | collective-permute-start | bytes 6152 | tf_op jit(solution)/shard_map/ppermute | solution.py:96
  88.9 1.0 %collective-permute-start = (f32[256,2]{0,1:T(2,128)S(1)}, f32[256,2]{0,1:T(2,128)S(1)}, u32[]{:S(2)}, u32[]{:S(2)}) collective-permute-start(f32[256,2]{0,1:T(2,128)S(1)} %bitcast.71), channel_id=1, source_target_pairs={{0,1},{1,2},{2,3},{3,0},{4,5},{5,6},{6,7},{7,4},{8,9},{9,10},{10,1... | collective-permute-start | bytes 6152 | tf_op jit(solution)/shard_map/ppermute | solution.py:96
  89.9 0.3 collective-permute-done.2
  90.2 3.2 %collective-permute-done.1 = f32[256,2]{0,1:T(2,128)S(1)} collective-permute-done((f32[256,2]{0,1:T(2,128)S(1)}, f32[256,2]{0,1:T(2,128)S(1)}, u32[]{:S(2)}, u32[]{:S(2)}) %collective-permute-start.1) | collective-permute-done | bytes 2080 | tf_op jit(solution)/shard_map/ppermute | solution.py:96
  93.4 0.9 collective-permute-done
  94.3 0.6 fusion.39
  (78 shorter events, 5.1 us)
Async XLA Ops:
  0.6 2.9 %copy-start = (s32[8,8,2]{1,2,0:T(2,128)S(1)}, s32[8,8,2]{1,2,0:T(2,128)}, u32[]{:S(2)}) copy-start(s32[8,8,2]{1,2,0:T(2,128)} %param.15) | copy-start | bytes 1540
  0.6 9.9 %copy-start.1 = (f32[16,64,512]{2,1,0:T(8,128)S(1)}, f32[16,64,512]{2,1,0:T(8,128)}, u32[]{:S(2)}) copy-start(f32[16,64,512]{2,1,0:T(8,128)} %param.9) | copy-start | bytes 6291460
  5.3 11.4 %all-to-all-start = ((f32[48,8,128]{2,0,1:T(8,128)}), f32[48,8,128]{2,0,1:T(8,128)S(1)}, u32[]{:S(2)}, u32[]{:S(2)}) async-start(f32[48,8,128]{2,0,1:T(8,128)} %copy.59), calls=%async_computation | async-start | bytes 393216 | tf_op jit(solution)/shard_map/all_to_all | solution.py:45
  10.5 2.4 %copy-start.5 = (s32[16]{0:T(128)S(1)}, s32[16]{0:T(128)}, u32[]{:S(2)}) copy-start(s32[16]{0:T(128)} %param.13) | copy-start | bytes 196
  19.6 6.2 %copy-start.2 = (f32[48,1024]{1,0:T(8,128)S(1)}, f32[48,1024]{1,0:T(8,128)}, u32[]{:S(2)}) copy-start(f32[48,1024]{1,0:T(8,128)} %param.10) | copy-start | bytes 589828
  38.5 6.2 %copy-start.3 = (f32[48,1024]{1,0:T(8,128)S(1)}, f32[48,1024]{1,0:T(8,128)}, u32[]{:S(2)}) copy-start(f32[48,1024]{1,0:T(8,128)} %param.11) | copy-start | bytes 589828
  44.9 4.4 %copy-start.4 = (s32[16,8]{0,1:T(8,128)S(1)}, s32[16,8]{0,1:T(8,128)}, u32[]{:S(2)}) copy-start(s32[16,8]{0,1:T(8,128)} %param.14) | copy-start | bytes 1540
  53.3 9.5 %all-to-all-start.2 = ((f32[48,8,128]{2,0,1:T(8,128)}), f32[48,8,128]{2,0,1:T(8,128)S(1)}, u32[]{:S(2)}, u32[]{:S(2)}) async-start(f32[48,8,128]{2,0,1:T(8,128)} %copy.74), calls=%async_computation.2 | async-start | bytes 393216 | tf_op jit(solution)/shard_map/all_to_all | solution.py:45
  72.7 12.3 %copy-start.6 = (f32[48]{0:T(128)S(1)}, f32[48]{0:T(128)}, u32[]{:S(2)}) copy-start(f32[48]{0:T(128)} %param.12) | copy-start | bytes 580
  73.4 9.5 %all-to-all-start.3 = ((f32[48,8,128]{2,0,1:T(8,128)}), f32[48,8,128]{2,0,1:T(8,128)S(1)}, u32[]{:S(2)}, u32[]{:S(2)}) async-start(f32[48,8,128]{2,0,1:T(8,128)} %copy.81), calls=%async_computation.3 | async-start | bytes 393216 | tf_op jit(solution)/shard_map/all_to_all | solution.py:45
  85.2 5.0 %collective-permute-start.2 = (f32[256,2]{0,1:T(2,128)S(1)}, f32[256,2]{0,1:T(2,128)S(1)}, u32[]{:S(2)}, u32[]{:S(2)}) collective-permute-start(f32[256,2]{0,1:T(2,128)S(1)} %bitcast.69), channel_id=1, source_target_pairs={{0,3},{1,0},{2,1},{3,2},{4,7},{5,4},{6,5},{7,6},{8,11},{9,8},{10,9... | collective-permute-start | bytes 6152 | tf_op jit(solution)/shard_map/ppermute | solution.py:96
  88.9 4.5 %collective-permute-start.1 = (f32[256,2]{0,1:T(2,128)S(1)}, f32[256,2]{0,1:T(2,128)S(1)}, u32[]{:S(2)}, u32[]{:S(2)}) collective-permute-start(f32[256,2]{0,1:T(2,128)S(1)} %bitcast.70), channel_id=1, source_target_pairs={{0,2},{1,3},{2,0},{3,1},{4,6},{5,7},{6,4},{7,5},{8,10},{9,11},{10,... | collective-permute-start | bytes 6152 | tf_op jit(solution)/shard_map/ppermute | solution.py:96
  88.9 5.4 %collective-permute-start = (f32[256,2]{0,1:T(2,128)S(1)}, f32[256,2]{0,1:T(2,128)S(1)}, u32[]{:S(2)}, u32[]{:S(2)}) collective-permute-start(f32[256,2]{0,1:T(2,128)S(1)} %bitcast.71), channel_id=1, source_target_pairs={{0,1},{1,2},{2,3},{3,0},{4,5},{5,6},{6,7},{7,4},{8,9},{9,10},{10,1... | collective-permute-start | bytes 6152 | tf_op jit(solution)/shard_map/ppermute | solution.py:96

commit v2 on v0

v2 whole, which is shorter than its diff:
```python
import jax
import jax.numpy as jnp
from jax import lax
from jax.experimental import pallas as pl
from jax.experimental.pallas import tpu as pltpu
from jax.sharding import PartitionSpec as P


def shift_pairs(count, shift):
    return [(j, (j + shift) % count) for j in range(count)]


def split_bf16(x):
    high = x.astype(jnp.bfloat16)
    low = (x - high.astype(jnp.float32)).astype(jnp.bfloat16)
    return high, low


def dot3(a, b):
    a_high, a_low = split_bf16(a)
    b_high, b_low = split_bf16(b)

    def one(u, v):
        return jnp.dot(u, v, preferred_element_type=jnp.float32)

    return one(a_high, b_high) + one(a_low, b_high) + one(a_high, b_low)


def forward_kernel(col_ref, table_ref, turn_ref, out_ref):
    blocks, slots = col_ref.shape
    block_len = table_ref.shape[1]
    for n in range(blocks):
        gathered = jnp.concatenate([table_ref[col_ref[n, s]] for s in range(slots)], axis=0)
        out_ref[n * block_len : (n + 1) * block_len, :] = dot3(turn_ref[n], gathered)


def adjoint_kernel(col_ref, ratio_ref, turn_ref, out_ref):
    blocks, slots = col_ref.shape
    block_len = ratio_ref.shape[0] // blocks
    out_ref[...] = jnp.zeros(out_ref.shape, out_ref.dtype)
    for n in range(blocks):
        terms = dot3(turn_ref[n], ratio_ref[n * block_len : (n + 1) * block_len, :])
        for s in range(slots):
            b = col_ref[n, s]
            out_ref[b] = out_ref[b] + terms[s * block_len : (s + 1) * block_len, :]


def local(cost, turn_weight, exit_value, demand, dest_weight, slot_count, col_ref, send_blocks):
    blocks = col_ref.shape[0]
    slot_total = col_ref.shape[1]
    block_len = turn_weight.shape[1]
    columns = exit_value.shape[0]
    capacity = send_blocks.shape[2]
    partitions = lax.axis_size("dom")
    my_part = lax.axis_index("dom")
    table_blocks = blocks + partitions * capacity
    own_len = blocks * block_len
    live = jnp.arange(slot_total, dtype=jnp.int32)[None, :] < slot_count[:, None]
    turn_matrix = turn_weight * jnp.repeat(live.astype(jnp.float32), block_len, axis=1)[:, None, :]
    turn_t = turn_matrix.transpose(0, 2, 1)
    link_scale = jnp.exp(-cost)[:, None]
    outbound = lax.dynamic_index_in_dim(send_blocks, my_part, 0, keepdims=False).reshape(-1)
    smem = pl.BlockSpec(memory_space=pltpu.SMEM)
    vmem = pl.BlockSpec(memory_space=pltpu.VMEM)
    forward = pl.pallas_call(
        forward_kernel,
        out_shape=jax.ShapeDtypeStruct((own_len, columns), jnp.float32),
        in_specs=[smem, vmem, vmem],
        out_specs=vmem,
    )
    adjoint = pl.pallas_call(
        adjoint_kernel,
        out_shape=jax.ShapeDtypeStruct((table_blocks, block_len, columns), jnp.float32),
        in_specs=[smem, vmem, vmem],
        out_specs=vmem,
    )

    def exchange(pieces):
        shaped = pieces.reshape(partitions, capacity * block_len, columns)
        got = lax.all_to_all(shaped, "dom", split_axis=0, concat_axis=0, tiled=True)
        return got.reshape(partitions * capacity, block_len, columns)

    exit_t = exit_value.T
    demand_t = demand.T
    value = exit_t
    for sweep in range(2):
        weighted = (value * link_scale).reshape(blocks, block_len, columns)
        received = exchange(weighted[outbound])
        table = jnp.concatenate([weighted, received], axis=0)
        value = forward(col_ref, table, turn_matrix) + exit_t
    load = demand_t
    back = demand_t
    for sweep in range(2):
        ratio = load / value
        totals = adjoint(col_ref, ratio, turn_t)
        returned = exchange(totals[blocks:])
        owned = totals[:blocks].at[outbound].add(returned)
        back = owned.reshape(own_len, columns) * link_scale
        load = value * back + demand_t
    dest_total = columns * lax.axis_size("dest")
    flow_part = jnp.sum(load, axis=1) / dest_total
    grad_part = -jnp.sum(dest_weight[None, :] * value * back, axis=1) / dest_total
    stacked = jnp.stack([flow_part, grad_part], axis=1)
    dest_n = lax.axis_size("dest")
    me = lax.axis_index("dest")
    parts = stacked.reshape(dest_n, -1, 2)
    both = lax.dynamic_index_in_dim(parts, me, 0, keepdims=False)
    for shift in range(1, dest_n):
        send = lax.dynamic_index_in_dim(parts, (me + shift) % dest_n, 0, keepdims=False)
        both = both + lax.ppermute(send, "dest", shift_pairs(dest_n, shift))
    return (both[:, 0], both[:, 1])


def solution(mesh):
    placed = (
        P("dom"),
        P("dom", None, None),
        P("dest", "dom"),
        P("dest", "dom"),
        P("dest"),
        P("dom"),
        P("dom", None),
        P(),
    )
    return jax.shard_map(
        local,
        mesh=mesh,
        in_specs=placed,
        out_specs=(P(("dom", "dest")), P(("dom", "dest"))),
        check_vma=False,
    )
```

time: 127 us -> 92.3 us (0.73)
  matrix products: 30.5 us -> 0 us
  blocking collectives: 29.3 us -> 0 us
  Pallas kernels: 0 us -> 18.3 us
  other arithmetic: 30.4 us -> 14.1 us
  waiting for transfers between devices: 9.69 us -> 21.5 us
  starting transfers between devices: 8.59 us -> 20 us
    dot_general x4 -> x0, matrix products: 30.5 us -> none  [the longest x2 15.6 us: local(): jnp.einsum('dnsj,nisj->dni', picked, turn_matrix, precision=lax.Precision...]
    scatter-add x4 -> x2, other arithmetic: 28.3 us -> 2.89 us  [local(): owned = totals[:blocks].at[outbound].add(returned)]
    pallas_call x0 -> x4, Pallas kernels: none -> 18.3 us  [the longest x2 10.3 us: local(): totals = adjoint(col_ref, ratio, turn_t)]
    all_to_all x2 -> x0, blocking collectives: 17.2 us -> none  [the longest x1 8.6 us: local(): lax.all_to_all(forward_outgoing, 'dom', split_axis=1, concat_axis=1, tile...]
    psum x1 -> x0, blocking collectives: 12.1 us -> none  [local(): flow_all, grad_all = lax.psum((flow_part, grad_part), 'dest')]
    all_to_all x2 -> x4, waiting for transfers between devices: 9.69 us -> 17.1 us  [exchange(): got = lax.all_to_all(shaped, 'dom', split_axis=0, concat_axis=0, tiled=True)]
    all_to_all x2 -> x4, starting transfers between devices: 8.59 us -> 15.4 us  [exchange(): got = lax.all_to_all(shaped, 'dom', split_axis=0, concat_axis=0, tiled=True)]
    ppermute x0 -> x3, starting transfers between devices: none -> 4.66 us  [local(): both = both + lax.ppermute(send, 'dest', shift_pairs(dest_n, shift))]
  transfers between devices with their start and end apart: 2 -> 7, of which waited for: 2 -> 7; matrix products, arithmetic and copies ran while one was open for 2% -> 8% of each run, Pallas kernels for 0% -> 0%
where the time goes in v2:
time: 92.3 us; the launch traced here: 91.4 us
  waiting for transfers between devices  21.5 us (23%)
  starting transfers between devices  20 us (22%)
  Pallas kernels  18.3 us (20%)
  local copies, waits for them, and re-layouts  16.5 us (18%)
  other arithmetic  14.1 us (15%)
  between operations  0.96 us (1%)
    all_to_all x4, waiting for transfers between devices, exchange(): got = lax.all_to_all(shaped, 'dom', split_axis=0, concat_axis=0, tiled=True)  17.1 us
    all_to_all x4, starting transfers between devices, exchange(): got = lax.all_to_all(shaped, 'dom', split_axis=0, concat_axis=0, tiled=True)  15.4 us
    pallas_call x2, Pallas kernels, local(): totals = adjoint(col_ref, ratio, turn_t)  10.3 us
    pallas_call x2, Pallas kernels, local(): value = forward(col_ref, table, turn_matrix) + exit_t  8.07 us
    ppermute x3, starting transfers between devices, local(): both = both + lax.ppermute(send, 'dest', shift_pairs(dest_n, shift))  4.66 us
    reshape x4, local copies, waits for them, and re-layouts, exchange(): shaped = pieces.reshape(partitions, capacity * block_len, columns)  4.48 us
    ppermute x3, waiting for transfers between devices, local(): both = both + lax.ppermute(send, 'dest', shift_pairs(dest_n, shift))  4.38 us
    mul x1, other arithmetic, local(): turn_weight * jnp.repeat(live.astype(jnp.float32), block_len, axis=1)[:,...  3.19 us
  transfers between devices with their start and end apart: 7, of which 7 were waited for; matrix products, arithmetic and copies ran while one was open for 8% of the time, Pallas kernels for 0%

profile of v2, /device:TPU:0, one launch (start us, length us, event | category | flops | bytes accessed | tf_op | source)
XLA Modules:
  0.0 91.4 jit_solution(17356104227999632210)
XLA Ops:
  0.7 1.1 %copy.66 = f32[48,1024]{0,1:T(8,128)S(1)} copy(f32[48,1024]{1,0:T(8,128)} %param.10) | data formatting | bytes 393216 | tf_op args[2]
  3.5 0.9 copy.68
  4.4 5.2 %all-to-all-start = ((f32[8,128,48]{1,2,0:T(8,128)}), f32[8,128,48]{1,2,0:T(8,128)S(1)}, u32[]{:S(2)}, u32[]{:S(2)}) async-start(f32[8,128,48]{1,2,0:T(8,128)} %copy.68), calls=%async_computation | async-start | bytes 393216 | tf_op jit(solution)/shard_map/all_to_all | solution.py:80
  10.5 3.2 %broadcast_multiply_fusion.turn_ref = f32[16,64,512]{2,1,0:T(8,128)} fusion(f32[16,64,512]{2,1,0:T(8,128)} %param.9, f32[16,512]{1,0:T(8,128)S(1)} %mul.55), kind=kLoop, calls=%fused_computation.6 | loop fusion | flops 524288 | bytes 4227072 | tf_op jit(solution)/shard_map/mul | solution.py:59
  13.6 2.1 %all-to-all-done = f32[8,128,48]{1,2,0:T(8,128)S(1)} async-done(((f32[8,128,48]{1,2,0:T(8,128)}), f32[8,128,48]{1,2,0:T(8,128)S(1)}, u32[]{:S(2)}, u32[]{:S(2)}) %all-to-all-start) | async-done | bytes 196640 | tf_op jit(solution)/shard_map/all_to_all | solution.py:80
  16.0 1.1 %pad_maximum_fusion.table_ref = f32[32,64,48]{2,1,0:T(8,128)} fusion(f32[16,64,48]{2,1,0:T(8,128)S(1)} %bitcast.69, f32[16,64,48]{2,1,0:T(8,128)S(1)} %bitcast.62), kind=kLoop, calls=%fused_computation.4 | loop fusion | flops 98304 | bytes 786432 | tf_op jit(solution)/shard_map/concatenate | solution.py:89
  17.0 4.0 %shard_map.95 = f32[1024,48]{1,0:T(8,128)} custom-call(s32[16,8]{1,0:T(8,128)} %copy.73.col_ref, f32[32,64,48]{2,1,0:T(8,128)} %pad_maximum_fusion.table_ref, f32[16,64,512]{2,1,0:T(8,128)} %broadcast_multiply_fusion.turn_ref), custom_call_target="tpu_custom_call" | custom-call | tf_op jit(solution)/shard_map/pallas_call | solution.py:90
  21.1 1.4 %fusion.4 = f32[1024,48]{1,0:T(8,128)S(1)} fusion(f32[1024,48]{1,0:T(8,128)} %shard_map.95, f32[48,1024]{0,1:T(8,128)S(1)} %copy.66, f32[1024]{0:T(1024)S(1)} %negate_exponential_fusion), kind=kLoop, calls=%fused_computation.18 | loop fusion | flops 98304 | bytes 593920 | tf_op jit(solution)/shard_map/mul | solution.py:87
  22.5 1.4 %gather_fusion.1 = f32[16,64,48]{2,1,0:T(8,128)} fusion(f32[16,64,48]{2,1,0:T(8,128)S(1)} %bitcast.63, s32[1024]{0:T(1024)S(1)} %pad_clamp_fusion), kind=kCustom, calls=%fused_computation.1 | custom fusion | bytes 393280 | tf_op jit(solution)/shard_map/gather | solution.py:88
  23.8 1.9 %copy.71 = f32[8,128,48]{1,2,0:T(8,128)} copy(f32[8,128,48]{2,1,0:T(8,128)} %bitcast.65) | data formatting | bytes 393216 | tf_op jit(solution)/shard_map/reshape | solution.py:79
  25.7 3.4 %all-to-all-start.1 = ((f32[8,128,48]{1,2,0:T(8,128)}), f32[8,128,48]{1,2,0:T(8,128)S(1)}, u32[]{:S(2)}, u32[]{:S(2)}) async-start(f32[8,128,48]{1,2,0:T(8,128)} %copy.71), calls=%async_computation.1 | async-start | bytes 393216 | tf_op jit(solution)/shard_map/all_to_all | solution.py:80
  29.2 2.7 %copy.75 = f32[16,64,512]{1,2,0:T(8,128)} copy(f32[16,64,512]{2,1,0:T(8,128)S(1)} %copy-done.1) | data formatting | bytes 4194304 | tf_op jit(solution)/shard_map/mul | solution.py:59
  32.1 3.2 %all-to-all-done.1 = f32[8,128,48]{1,2,0:T(8,128)S(1)} async-done(((f32[8,128,48]{1,2,0:T(8,128)}), f32[8,128,48]{1,2,0:T(8,128)S(1)}, u32[]{:S(2)}, u32[]{:S(2)}) %all-to-all-start.1) | async-done | bytes 196640 | tf_op jit(solution)/shard_map/all_to_all | solution.py:80
  35.5 1.1 %pad_maximum_fusion.1.table_ref = f32[32,64,48]{2,1,0:T(8,128)} fusion(f32[16,64,48]{2,1,0:T(8,128)S(1)} %bitcast.70, f32[16,64,48]{2,1,0:T(8,128)S(1)} %bitcast.64), kind=kLoop, calls=%fused_computation.5 | loop fusion | flops 98304 | bytes 786432 | tf_op jit(solution)/shard_map/concatenate | solution.py:89
  36.5 4.0 %shard_map.96 = f32[1024,48]{1,0:T(8,128)} custom-call(s32[16,8]{1,0:T(8,128)} %copy.73.col_ref, f32[32,64,48]{2,1,0:T(8,128)} %pad_maximum_fusion.1.table_ref, f32[16,64,512]{2,1,0:T(8,128)} %broadcast_multiply_fusion.turn_ref), custom_call_target="tpu_custom_call" | custom-call | tf_op jit(solution)/shard_map/pallas_call | solution.py:90
  40.6 2.0 %bitcast_divide_fusion = (f32[1024,48]{1,0:T(8,128)}, f32[1024,48]{1,0:T(8,128)S(1)}) fusion(f32[48,1024]{0,1:T(8,128)S(1)} %copy.74, f32[1024,48]{1,0:T(8,128)} %shard_map.96, f32[48,1024]{0,1:T(8,128)S(1)} %copy.66), kind=kLoop, calls=%fused_computation.13 | loop fusion | flops 98304 | bytes 983040 | tf_op jit(solution)/shard_map/div | solution.py:94
  42.5 5.1 %shard_map.97 = f32[32,64,48]{2,1,0:T(8,128)} custom-call(s32[16,8]{1,0:T(8,128)} %copy.73.col_ref, f32[1024,48]{1,0:T(8,128)} %get-tuple-element.4.ratio_ref, f32[16,512,64]{2,1,0:T(8,128)} %bitcast.59), custom_call_target="tpu_custom_call" | custom-call | tf_op jit(solution)/shard_map/pallas_call | solution.py:95
  47.7 1.3 %fusion.10 = (f32[16,64,48]{2,1,0:T(8,128)S(1)}, f32[16,64,48]{2,1,0:T(8,128)S(1)}) fusion(f32[32,64,48]{2,1,0:T(8,128)} %shard_map.97), kind=kLoop, calls=%fused_computation.42 | loop fusion | bytes 786432 | tf_op jit(solution)/shard_map/slice | solution.py:96
  48.9 0.9 copy.77
  49.8 3.4 %all-to-all-start.2 = ((f32[8,128,48]{1,2,0:T(8,128)}), f32[8,128,48]{1,2,0:T(8,128)S(1)}, u32[]{:S(2)}, u32[]{:S(2)}) async-start(f32[8,128,48]{1,2,0:T(8,128)} %copy.77), calls=%async_computation.2 | async-start | bytes 393216 | tf_op jit(solution)/shard_map/all_to_all | solution.py:80
  53.4 5.9 %all-to-all-done.2 = f32[8,128,48]{1,2,0:T(8,128)S(1)} async-done(((f32[8,128,48]{1,2,0:T(8,128)}), f32[8,128,48]{1,2,0:T(8,128)S(1)}, u32[]{:S(2)}, u32[]{:S(2)}) %all-to-all-start.2) | async-done | bytes 196640 | tf_op jit(solution)/shard_map/all_to_all | solution.py:80
  59.7 1.4 %scatter_fusion = f32[16,64,48]{1,2,0:T(8,128)S(1)} fusion(f32[16,64,48]{1,2,0:T(8,128)S(1)} %copy.79, s32[16]{0:T(128)S(1)} %fusion.8, f32[16,64,48]{1,2,0:T(8,128)S(1)} %copy.80), kind=kCustom, calls=%fused_computation.2 | custom fusion | flops 49152 | bytes 589888 | tf_op jit(solution)/shard_map/scatter-add | solution.py:97
  61.3 1.1 %fusion.2.ratio_ref = f32[1024,48]{1,0:T(8,128)} fusion(f32[1024,48]{1,0:T(8,128)S(1)} %get-tuple-element.5, f32[16,64,48]{2,1,0:T(8,128)S(1)} %copy.81, f32[48,1024]{0,1:T(8,128)S(1)} %copy.74, f32[1024]{0:T(1024)S(1)} %negate_exponential_fusion), kind=kLoop, calls=%fused_computation.11 | loop fusion | flops 196608 | bytes 790528 | tf_op jit(solution)/shard_map/div | solution.py:94
  62.4 5.1 %shard_map.98 = f32[32,64,48]{2,1,0:T(8,128)} custom-call(s32[16,8]{1,0:T(8,128)} %copy.73.col_ref, f32[1024,48]{1,0:T(8,128)} %fusion.2.ratio_ref, f32[16,512,64]{2,1,0:T(8,128)} %bitcast.60), custom_call_target="tpu_custom_call" | custom-call | tf_op jit(solution)/shard_map/pallas_call | solution.py:95
  67.5 1.3 %fusion.9 = (f32[16,64,48]{2,1,0:T(8,128)S(1)}, f32[16,64,48]{2,1,0:T(8,128)S(1)}) fusion(f32[32,64,48]{2,1,0:T(8,128)} %shard_map.98), kind=kLoop, calls=%fused_computation.41 | loop fusion | bytes 786432 | tf_op jit(solution)/shard_map/slice | solution.py:96
  69.7 3.4 %all-to-all-start.3 = ((f32[8,128,48]{1,2,0:T(8,128)}), f32[8,128,48]{1,2,0:T(8,128)S(1)}, u32[]{:S(2)}, u32[]{:S(2)}) async-start(f32[8,128,48]{1,2,0:T(8,128)} %copy.83), calls=%async_computation.3 | async-start | bytes 393216 | tf_op jit(solution)/shard_map/all_to_all | solution.py:80
  73.3 5.9 %all-to-all-done.3 = f32[8,128,48]{1,2,0:T(8,128)S(1)} async-done(((f32[8,128,48]{1,2,0:T(8,128)}), f32[8,128,48]{1,2,0:T(8,128)S(1)}, u32[]{:S(2)}, u32[]{:S(2)}) %all-to-all-start.3) | async-done | bytes 196640 | tf_op jit(solution)/shard_map/all_to_all | solution.py:80
  79.5 1.4 %scatter_fusion.1 = f32[16,64,48]{1,2,0:T(8,128)S(1)} fusion(f32[16,64,48]{1,2,0:T(8,128)S(1)} %copy.85, s32[16]{0:T(128)S(1)} %fusion.8, f32[16,64,48]{1,2,0:T(8,128)S(1)} %copy.86), kind=kCustom, calls=%fused_computation.3 | custom fusion | flops 49152 | bytes 589888 | tf_op jit(solution)/shard_map/scatter-add | solution.py:97
  81.8 3.7 %collective-permute-start.2 = (f32[256,2]{0,1:T(2,128)S(1)}, f32[256,2]{0,1:T(2,128)S(1)}, u32[]{:S(2)}, u32[]{:S(2)}) collective-permute-start(f32[256,2]{0,1:T(2,128)S(1)} %bitcast.71), channel_id=1, source_target_pairs={{0,3},{1,0},{2,1},{3,2},{4,7},{5,4},{6,5},{7,6},{8,11},{9,8},{10,9... | collective-permute-start | bytes 6152 | tf_op jit(solution)/shard_map/ppermute | solution.py:110
  85.5 1.0 %collective-permute-start = (f32[256,2]{0,1:T(2,128)S(1)}, f32[256,2]{0,1:T(2,128)S(1)}, u32[]{:S(2)}, u32[]{:S(2)}) collective-permute-start(f32[256,2]{0,1:T(2,128)S(1)} %bitcast.73), channel_id=1, source_target_pairs={{0,1},{1,2},{2,3},{3,0},{4,5},{5,6},{6,7},{7,4},{8,9},{9,10},{10,1... | collective-permute-start | bytes 6152 | tf_op jit(solution)/shard_map/ppermute | solution.py:110
  86.8 3.2 %collective-permute-done.1 = f32[256,2]{0,1:T(2,128)S(1)} collective-permute-done((f32[256,2]{0,1:T(2,128)S(1)}, f32[256,2]{0,1:T(2,128)S(1)}, u32[]{:S(2)}, u32[]{:S(2)}) %collective-permute-start.1) | collective-permute-done | bytes 2080 | tf_op jit(solution)/shard_map/ppermute | solution.py:110
  90.0 0.9 collective-permute-done
  (52 shorter events, 6.9 us)
Async XLA Ops:
  0.6 1.9 %copy-start = (s32[8,8,2]{1,2,0:T(2,128)S(1)}, s32[8,8,2]{1,2,0:T(2,128)}, u32[]{:S(2)}) copy-start(s32[8,8,2]{1,2,0:T(2,128)} %param.15) | copy-start | bytes 1540
  0.6 8.9 %copy-start.3 = (s32[16,8]{0,1:T(8,128)S(1)}, s32[16,8]{0,1:T(8,128)}, u32[]{:S(2)}) copy-start(s32[16,8]{0,1:T(8,128)} %param.14) | copy-start | bytes 1540
  0.7 9.6 %copy-start.5 = (s32[16]{0:T(128)S(1)}, s32[16]{0:T(128)}, u32[]{:S(2)}) copy-start(s32[16]{0:T(128)} %param.13) | copy-start | bytes 196
  4.4 11.4 %all-to-all-start = ((f32[8,128,48]{1,2,0:T(8,128)}), f32[8,128,48]{1,2,0:T(8,128)S(1)}, u32[]{:S(2)}, u32[]{:S(2)}) async-start(f32[8,128,48]{1,2,0:T(8,128)} %copy.68), calls=%async_computation | async-start | bytes 393216 | tf_op jit(solution)/shard_map/all_to_all | solution.py:80
  21.1 8.1 %copy-start.1 = (f32[16,64,512]{2,1,0:T(8,128)S(1)}, f32[16,64,512]{2,1,0:T(8,128)}, u32[]{:S(2)}) copy-start(f32[16,64,512]{2,1,0:T(8,128)} %broadcast_multiply_fusion.turn_ref) | copy-start | bytes 6291460
  25.7 9.5 %all-to-all-start.1 = ((f32[8,128,48]{1,2,0:T(8,128)}), f32[8,128,48]{1,2,0:T(8,128)S(1)}, u32[]{:S(2)}, u32[]{:S(2)}) async-start(f32[8,128,48]{1,2,0:T(8,128)} %copy.71), calls=%async_computation.1 | async-start | bytes 393216 | tf_op jit(solution)/shard_map/all_to_all | solution.py:80
  29.2 2.7 %copy-start.2 = (f32[48,1024]{1,0:T(8,128)S(1)}, f32[48,1024]{1,0:T(8,128)}, u32[]{:S(2)}) copy-start(f32[48,1024]{1,0:T(8,128)} %param.11) | copy-start | bytes 589828
  49.8 9.5 %all-to-all-start.2 = ((f32[8,128,48]{1,2,0:T(8,128)}), f32[8,128,48]{1,2,0:T(8,128)S(1)}, u32[]{:S(2)}, u32[]{:S(2)}) async-start(f32[8,128,48]{1,2,0:T(8,128)} %copy.77), calls=%async_computation.2 | async-start | bytes 393216 | tf_op jit(solution)/shard_map/all_to_all | solution.py:80
  69.7 9.5 %all-to-all-start.3 = ((f32[8,128,48]{1,2,0:T(8,128)}), f32[8,128,48]{1,2,0:T(8,128)S(1)}, u32[]{:S(2)}, u32[]{:S(2)}) async-start(f32[8,128,48]{1,2,0:T(8,128)} %copy.83), calls=%async_computation.3 | async-start | bytes 393216 | tf_op jit(solution)/shard_map/all_to_all | solution.py:80
  73.3 7.9 %copy-start.4 = (f32[48]{0:T(128)S(1)}, f32[48]{0:T(128)}, u32[]{:S(2)}) copy-start(f32[48]{0:T(128)} %param.12) | copy-start | bytes 580
  81.8 5.0 %collective-permute-start.2 = (f32[256,2]{0,1:T(2,128)S(1)}, f32[256,2]{0,1:T(2,128)S(1)}, u32[]{:S(2)}, u32[]{:S(2)}) collective-permute-start(f32[256,2]{0,1:T(2,128)S(1)} %bitcast.71), channel_id=1, source_target_pairs={{0,3},{1,0},{2,1},{3,2},{4,7},{5,4},{6,5},{7,6},{8,11},{9,8},{10,9... | collective-permute-start | bytes 6152 | tf_op jit(solution)/shard_map/ppermute | solution.py:110
  85.5 4.5 %collective-permute-start.1 = (f32[256,2]{0,1:T(2,128)S(1)}, f32[256,2]{0,1:T(2,128)S(1)}, u32[]{:S(2)}, u32[]{:S(2)}) collective-permute-start(f32[256,2]{0,1:T(2,128)S(1)} %bitcast.72), channel_id=1, source_target_pairs={{0,2},{1,3},{2,0},{3,1},{4,6},{5,7},{6,4},{7,5},{8,10},{9,11},{10,... | collective-permute-start | bytes 6152 | tf_op jit(solution)/shard_map/ppermute | solution.py:110
  85.5 5.4 %collective-permute-start = (f32[256,2]{0,1:T(2,128)S(1)}, f32[256,2]{0,1:T(2,128)S(1)}, u32[]{:S(2)}, u32[]{:S(2)}) collective-permute-start(f32[256,2]{0,1:T(2,128)S(1)} %bitcast.73), channel_id=1, source_target_pairs={{0,1},{1,2},{2,3},{3,0},{4,5},{5,6},{6,7},{7,4},{8,9},{9,10},{10,1... | collective-permute-start | bytes 6152 | tf_op jit(solution)/shard_map/ppermute | solution.py:110

commit v3 on v2

v3 whole, which is shorter than its diff:
```python
import jax
import jax.numpy as jnp
from jax import lax
from jax.experimental import pallas as pl
from jax.experimental.pallas import tpu as pltpu
from jax.sharding import PartitionSpec as P


def shift_pairs(count, shift):
    return [(j, (j + shift) % count) for j in range(count)]


def split_bf16(x):
    high = x.astype(jnp.bfloat16)
    low = (x - high.astype(jnp.float32)).astype(jnp.bfloat16)
    return high, low


def dot3(a, b):
    a_high, a_low = split_bf16(a)
    b_high, b_low = split_bf16(b)

    def one(u, v):
        return jnp.dot(u, v, preferred_element_type=jnp.float32)

    return one(a_high, b_high) + one(a_low, b_high) + one(a_high, b_low)


def live_factor(cnt_ref, n, s):
    return jnp.where(s < cnt_ref[n], 1.0, 0.0).astype(jnp.float32)


def add_returned(owned, out_idx_ref, returned_ref):
    block_len = owned.shape[1]
    capacity = out_idx_ref.shape[0] // returned_ref.shape[0]
    for p in range(returned_ref.shape[0]):
        got = returned_ref[p].T
        for c in range(capacity):
            b = out_idx_ref[p * capacity + c]
            owned[b] = owned[b] + got[c * block_len : (c + 1) * block_len, :]


def forward_kernel(with_send, cnt_ref, col_ref, out_idx_ref, value_ref, recv_ref, turn_ref,
                   scale_ref, exit_ref, *rest):
    if with_send:
        value_out, send_out, table = rest
    else:
        value_out, table = rest
    blocks = value_ref.shape[0]
    ghosts = out_idx_ref.shape[0]
    slots = col_ref.shape[1]
    block_len = value_ref.shape[1]
    capacity = ghosts // recv_ref.shape[0]
    table[0:blocks] = value_ref[...] * scale_ref[...]
    for p in range(recv_ref.shape[0]):
        table[blocks + p * capacity : blocks + (p + 1) * capacity] = recv_ref[p].T.reshape(
            capacity, block_len, -1
        )
    for n in range(blocks):
        pieces = [table[col_ref[n, s]] * live_factor(cnt_ref, n, s) for s in range(slots)]
        value_out[n] = dot3(turn_ref[n], jnp.concatenate(pieces, axis=0)) + exit_ref[n]
    if with_send:
        for p in range(send_out.shape[0]):
            rows = []
            for c in range(capacity):
                b = out_idx_ref[p * capacity + c]
                rows.append(value_out[b] * scale_ref[b])
            send_out[p] = jnp.concatenate(rows, axis=0).T


def adjoint_kernel(first, cnt_ref, col_ref, out_idx_ref, value_ref, demand_ref, scale_ref,
                   own_ref, returned_ref, turn_ref, own_out, ghost_out, ratio, totals):
    blocks = value_ref.shape[0]
    ghosts = out_idx_ref.shape[0]
    slots = col_ref.shape[1]
    block_len = value_ref.shape[1]
    capacity = ghosts // ghost_out.shape[0]
    if first:
        ratio[...] = demand_ref[...] / value_ref[...]
    else:
        totals[0:blocks] = own_ref[...]
        add_returned(totals, out_idx_ref, returned_ref)
        value = value_ref[...]
        load = value * (totals[0:blocks] * scale_ref[...]) + demand_ref[...]
        ratio[...] = load / value
    totals[...] = jnp.zeros(totals.shape, totals.dtype)
    for n in range(blocks):
        terms = dot3(turn_ref[n], ratio[n])
        for s in range(slots):
            b = col_ref[n, s]
            piece = terms[s * block_len : (s + 1) * block_len, :] * live_factor(cnt_ref, n, s)
            totals[b] = totals[b] + piece
    own_out[...] = totals[0:blocks]
    for p in range(ghost_out.shape[0]):
        part = totals[blocks + p * capacity : blocks + (p + 1) * capacity]
        ghost_out[p] = part.reshape(capacity * block_len, -1).T


def final_kernel(out_idx_ref, value_ref, demand_ref, scale_ref, own_ref, returned_ref, weight_ref,
                 flow_out, grad_out, owned):
    owned[...] = own_ref[...]
    add_returned(owned, out_idx_ref, returned_ref)
    value = value_ref[...]
    back = owned[...] * scale_ref[...]
    load = value * back + demand_ref[...]
    flow_out[...] = jnp.sum(load, axis=2, keepdims=True)
    grad_out[...] = jnp.sum(weight_ref[...] * value * back, axis=2, keepdims=True)


def local(cost, turn_weight, exit_value, demand, dest_weight, slot_count, col_ref, send_blocks):
    blocks = col_ref.shape[0]
    block_len = turn_weight.shape[1]
    columns = exit_value.shape[0]
    capacity = send_blocks.shape[2]
    partitions = lax.axis_size("dom")
    my_part = lax.axis_index("dom")
    ghosts = partitions * capacity
    own_len = blocks * block_len
    f32 = jnp.float32
    block_shape = (blocks, block_len, columns)
    ghost_shape = (partitions, columns, capacity * block_len)
    turn_t = turn_weight.transpose(0, 2, 1)
    scale = jnp.broadcast_to(jnp.exp(-cost).reshape(blocks, block_len, 1), block_shape)
    outbound = lax.dynamic_index_in_dim(send_blocks, my_part, 0, keepdims=False).reshape(-1)
    smem = pl.BlockSpec(memory_space=pltpu.SMEM)
    vmem = pl.BlockSpec(memory_space=pltpu.VMEM)
    scratch = pltpu.VMEM((blocks + ghosts, block_len, columns), f32)

    def forward(with_send):
        outs = [jax.ShapeDtypeStruct(block_shape, f32)]
        if with_send:
            outs.append(jax.ShapeDtypeStruct(ghost_shape, f32))
        return pl.pallas_call(
            lambda *refs: forward_kernel(with_send, *refs),
            out_shape=tuple(outs),
            in_specs=[smem, smem, smem] + [vmem] * 5,
            out_specs=tuple([vmem] * len(outs)),
            scratch_shapes=[scratch],
        )

    def adjoint(first):
        return pl.pallas_call(
            lambda *refs: adjoint_kernel(first, *refs),
            out_shape=(jax.ShapeDtypeStruct(block_shape, f32), jax.ShapeDtypeStruct(ghost_shape, f32)),
            in_specs=[smem, smem, smem] + [vmem] * 6,
            out_specs=(vmem, vmem),
            scratch_shapes=[pltpu.VMEM(block_shape, f32), scratch],
        )

    final = pl.pallas_call(
        final_kernel,
        out_shape=(
            jax.ShapeDtypeStruct((blocks, block_len, 1), f32),
            jax.ShapeDtypeStruct((blocks, block_len, 1), f32),
        ),
        in_specs=[smem] + [vmem] * 6,
        out_specs=(vmem, vmem),
        scratch_shapes=[pltpu.VMEM(block_shape, f32)],
    )

    def exchange(pieces):
        return lax.all_to_all(pieces, "dom", split_axis=0, concat_axis=0, tiled=True)

    exit_t = exit_value.T.reshape(block_shape)
    demand_t = demand.T.reshape(block_shape)
    idx = (slot_count, col_ref, outbound)
    first_send = (exit_value * jnp.exp(-cost)[None, :]).reshape(columns, blocks, block_len)[:, outbound, :]
    received = exchange(
        first_send.reshape(columns, partitions, capacity * block_len).transpose(1, 0, 2)
    )
    value, send = forward(True)(*idx, exit_t, received, turn_weight, scale, exit_t)
    received = exchange(send)
    (value,) = forward(False)(*idx, value, received, turn_weight, scale, exit_t)
    own, ghost = adjoint(True)(*idx, value, demand_t, scale, demand_t, demand_t[:1], turn_t)
    returned = exchange(ghost)
    own, ghost = adjoint(False)(*idx, value, demand_t, scale, own, returned, turn_t)
    returned = exchange(ghost)
    weight = dest_weight.reshape(1, 1, columns)
    flow_sum, grad_sum = final(outbound, value, demand_t, scale, own, returned, weight)
    dest_total = columns * lax.axis_size("dest")
    flow_part = flow_sum.reshape(own_len) / dest_total
    grad_part = -grad_sum.reshape(own_len) / dest_total
    stacked = jnp.stack([flow_part, grad_part], axis=1)
    dest_n = lax.axis_size("dest")
    me = lax.axis_index("dest")
    parts = stacked.reshape(dest_n, -1, 2)
    both = lax.dynamic_index_in_dim(parts, me, 0, keepdims=False)
    for shift in range(1, dest_n):
        send_part = lax.dynamic_index_in_dim(parts, (me + shift) % dest_n, 0, keepdims=False)
        both = both + lax.ppermute(send_part, "dest", shift_pairs(dest_n, shift))
    return (both[:, 0], both[:, 1])


def solution(mesh):
    placed = (
        P("dom"),
        P("dom", None, None),
        P("dest", "dom"),
        P("dest", "dom"),
        P("dest"),
        P("dom"),
        P("dom", None),
        P(),
    )
    return jax.shard_map(
        local,
        mesh=mesh,
        in_specs=placed,
        out_specs=(P(("dom", "dest")), P(("dom", "dest"))),
        check_vma=False,
    )
```

time: 92.3 us -> 82.6 us (0.89)
  other arithmetic: 14.1 us -> 3.21 us
  blocking collectives: 0 us -> 10.2 us
  waiting for transfers between devices: 21.5 us -> 14.8 us
  Pallas kernels: 18.3 us -> 23.8 us
  local copies, waits for them, and re-layouts: 16.5 us -> 11.6 us
  starting transfers between devices: 20 us -> 17.5 us
    all_to_all x0 -> x1, blocking collectives: none -> 10.2 us  [exchange(): lax.all_to_all(pieces, 'dom', split_axis=0, concat_axis=0, tiled=True)]
    pallas_call x4 -> x5, Pallas kernels: 18.3 us -> 23.8 us  [the longest x1 6.07 us: local(): adjoint(False)(*idx, value, demand_t, scale, own, returned, turn_t)]
    all_to_all x4 -> x3, waiting for transfers between devices: 17.1 us -> 12.5 us  [exchange(): lax.all_to_all(pieces, 'dom', split_axis=0, concat_axis=0, tiled=True)]
    reshape x8 -> x4, local copies, waits for them, and re-layouts: 4.98 us -> 1.09 us  [the longest x2 0.84 us: local(): first_send.reshape(columns, partitions, capacity * block_len)]
    mul x3 -> x1, other arithmetic: 4.78 us -> 0.95 us  [local(): exit_value * jnp.exp(-cost)[None, :]]
    unnamed x19 -> x25, local copies, waits for them, and re-layouts: 2.03 us -> 5.64 us
    all_to_all x4 -> x3, starting transfers between devices: 15.4 us -> 12 us  [exchange(): lax.all_to_all(pieces, 'dom', split_axis=0, concat_axis=0, tiled=True)]
    scatter-add x2 -> x0, other arithmetic: 2.89 us -> none  [local(): owned = totals[:blocks].at[outbound].add(returned)]
  transfers between devices with their start and end apart: 7 -> 6, of which waited for: 7 -> 5; matrix products, arithmetic and copies ran while one was open for 8% -> 7% of each run, Pallas kernels for 0% -> 0%
where the time goes in v3:
time: 82.6 us; the launch traced here: 82 us
  Pallas kernels  23.8 us (29%)
  starting transfers between devices  17.5 us (21%)
  waiting for transfers between devices  14.8 us (18%)
  local copies, waits for them, and re-layouts  11.6 us (14%)
  blocking collectives  10.2 us (12%)
  other arithmetic  3.21 us (4%)
  between operations  0.85 us (1%)
    all_to_all x3, waiting for transfers between devices, exchange(): lax.all_to_all(pieces, 'dom', split_axis=0, concat_axis=0, tiled=True)  12.5 us
    all_to_all x3, starting transfers between devices, exchange(): lax.all_to_all(pieces, 'dom', split_axis=0, concat_axis=0, tiled=True)  12 us
    all_to_all x1, blocking collectives, exchange(): lax.all_to_all(pieces, 'dom', split_axis=0, concat_axis=0, tiled=True)  10.2 us
    pallas_call x1, Pallas kernels, local(): adjoint(False)(*idx, value, demand_t, scale, own, returned, turn_t)  6.07 us
    pallas_call x1, Pallas kernels, local(): adjoint(True)(*idx, value, demand_t, scale, demand_t, demand_t[:1], turn_t)  5.68 us
    unnamed x25, local copies, waits for them, and re-layouts  5.64 us
    ppermute x3, starting transfers between devices, local(): both = both + lax.ppermute(send_part, 'dest', shift_pairs(dest_n, shift))  5.56 us
    pallas_call x1, Pallas kernels, local(): forward(True)(*idx, exit_t, received, turn_weight, scale, exit_t)  4.56 us
  transfers between devices with their start and end apart: 6, of which 5 were waited for; matrix products, arithmetic and copies ran while one was open for 7% of the time, Pallas kernels for 0%

profile of v3, /device:TPU:0, one launch (start us, length us, event | category | flops | bytes accessed | tf_op | source)
XLA Modules:
  0.0 82.0 jit_solution(9426477814006402765)
XLA Ops:
  0.7 0.6 copy-done
  1.5 0.7 negate_exponential_fusion
  2.2 0.9 %broadcast_multiply_fusion = f32[48,1024]{1,0:T(8,128)S(1)} fusion(f32[48,1024]{1,0:T(8,128)} %param.10, f32[1024]{0:T(1024)S(1)} %negate_exponential_fusion), kind=kLoop, calls=%fused_computation.4 | loop fusion | flops 49152 | bytes 397312 | tf_op jit(solution)/shard_map/mul | solution.py:167
  3.4 0.6 gather_fusion
  4.3 0.7 copy.51
  5.0 5.2 %all-to-all-start = ((f32[8,48,128]{2,1,0:T(8,128)}), f32[8,48,128]{2,1,0:T(8,128)S(1)}, u32[]{:S(2)}, u32[]{:S(2)}) async-start(f32[8,48,128]{2,1,0:T(8,128)} %bitcast.28), calls=%async_computation | async-start | bytes 393216 | tf_op jit(solution)/shard_map/all_to_all | solution.py:162
  10.2 0.6 reshape.92.refs_2_.out_idx_ref
  10.8 0.7 copy.37.refs_1_
  11.5 1.0 %copy.31 = f32[1024,48]{1,0:T(8,128)} copy(f32[1024,48]{0,1:T(8,128)S(1)} %bitcast.43) | data formatting | bytes 393216 | tf_op jit(solution)/shard_map/transpose | solution.py:164
  12.8 2.7 %copy.39 = f32[16,64,512]{1,2,0:T(8,128)} copy(f32[16,64,512]{2,1,0:T(8,128)S(1)} %copy-done.1) | data formatting | bytes 4194304 | tf_op args[1]
  15.5 0.9 %all-to-all-done.refs_4_ = f32[8,48,128]{2,1,0:T(8,128)S(1)} async-done(((f32[8,48,128]{2,1,0:T(8,128)}), f32[8,48,128]{2,1,0:T(8,128)S(1)}, u32[]{:S(2)}, u32[]{:S(2)}) %all-to-all-start) | async-done | bytes 196640 | tf_op jit(solution)/shard_map/all_to_all | solution.py:162
  16.4 1.0 %broadcast_in_dim.10.refs_6_.refs_5_.scale_ref = f32[16,64,48]{2,1,0:T(8,128)} broadcast(f32[16,64]{1,0:T(8,128)S(1)} %broadcast_in_dim.4), dimensions={0,1} | broadcast | bytes 200704 | tf_op jit(solution)/shard_map/broadcast_in_dim | solution.py:123
  17.4 4.6 %shard_map.95 = (f32[16,64,48]{2,1,0:T(8,128)}, f32[8,48,128]{2,1,0:T(8,128)}) custom-call(s32[16]{0:T(128)} %refs_0_.7, s32[16,8]{1,0:T(8,128)} %copy.37.refs_1_, s32[16]{0:T(128)} %reshape.92.refs_2_.out_idx_ref, f32[16,64,48]{2,1,0:T(8,128)} %bitcast.39, f32[8,48,128]{2,1,0:T(8,128)} %copy-done.3, f32[16,64,512]{2,1,0:T(8,128)} %refs_5_.3, ...), custom_call_target="tpu_custom_call" | custom-call | tf_op jit(solution)/shard_map/pallas_call | solution.py:171
  22.0 3.4 %all-to-all-start.1 = ((f32[8,48,128]{2,1,0:T(8,128)}), f32[8,48,128]{2,1,0:T(8,128)S(1)}, u32[]{:S(2)}, u32[]{:S(2)}) async-start(f32[8,48,128]{2,1,0:T(8,128)} %get-tuple-element.11), calls=%async_computation.1 | async-start | bytes 393216 | tf_op jit(solution)/shard_map/all_to_all | solution.py:162
  25.4 0.6 slice_bitcast_fusion.refs_7_
  26.0 5.5 %all-to-all-done.1.refs_4_ = f32[8,48,128]{2,1,0:T(8,128)S(1)} async-done(((f32[8,48,128]{2,1,0:T(8,128)}), f32[8,48,128]{2,1,0:T(8,128)S(1)}, u32[]{:S(2)}, u32[]{:S(2)}) %all-to-all-start.1) | async-done | bytes 196640 | tf_op jit(solution)/shard_map/all_to_all | solution.py:162
  31.5 0.7 copy-done.4
  32.2 4.5 %shard_map.96.refs_3_.value_ref = f32[16,64,48]{2,1,0:T(8,128)} custom-call(s32[16]{0:T(128)} %refs_0_.7, s32[16,8]{1,0:T(8,128)} %copy.37.refs_1_, s32[16]{0:T(128)} %reshape.92.refs_2_.out_idx_ref, f32[16,64,48]{2,1,0:T(8,128)} %get-tuple-element.10.refs_3_, f32[8,48,128]{2,1,0:T(8,128)} %copy-done.4, f32[16,64,512]{2,1,0:T(8,128)} %refs_5_.3, ...), custom_call_target="tpu_custom_call" | custom-call | tf_op jit(solution)/shard_map/pallas_call | solution.py:173
  36.7 5.7 %shard_map.97 = (f32[16,64,48]{2,1,0:T(8,128)}, f32[8,48,128]{2,1,0:T(8,128)}) custom-call(s32[16]{0:T(128)} %refs_0_.7, s32[16,8]{1,0:T(8,128)} %copy.37.refs_1_, s32[16]{0:T(128)} %reshape.92.refs_2_.out_idx_ref, f32[16,64,48]{2,1,0:T(8,128)} %shard_map.96.refs_3_.value_ref, f32[16,64,48]{2,1,0:T(8,128)} %bitcast.35, ...), custom_call_target="tpu_custom_call" | custom-call | tf_op jit(solution)/shard_map/pallas_call | solution.py:174
  42.3 10.2 %all_to_all.20.refs_7_ = f32[8,48,128]{2,1,0:T(8,128)} all-to-all(f32[8,48,128]{2,1,0:T(8,128)} %get-tuple-element.13), channel_id=1, replica_groups=mesh['dom'=8,'dest'=4] {'dom'}, dimensions={0} | all-to-all | bytes 393216 | tf_op jit(solution)/shard_map/all_to_all | solution.py:162
  52.5 6.1 %shard_map.98 = (f32[16,64,48]{2,1,0:T(8,128)}, f32[8,48,128]{2,1,0:T(8,128)}) custom-call(s32[16]{0:T(128)} %refs_0_.7, s32[16,8]{1,0:T(8,128)} %copy.37.refs_1_, s32[16]{0:T(128)} %reshape.92.refs_2_.out_idx_ref, f32[16,64,48]{2,1,0:T(8,128)} %shard_map.96.refs_3_.value_ref, f32[16,64,48]{2,1,0:T(8,128)} %bitcast.37, ...), custom_call_target="tpu_custom_call" | custom-call | tf_op jit(solution)/shard_map/pallas_call | solution.py:176
  58.6 3.4 %all-to-all-start.3 = ((f32[8,48,128]{2,1,0:T(8,128)}), f32[8,48,128]{2,1,0:T(8,128)S(1)}, u32[]{:S(2)}, u32[]{:S(2)}) async-start(f32[8,48,128]{2,1,0:T(8,128)} %get-tuple-element.15), calls=%async_computation.3 | async-start | bytes 393216 | tf_op jit(solution)/shard_map/all_to_all | solution.py:162
  62.1 6.1 %all-to-all-done.3.returned_ref = f32[8,48,128]{2,1,0:T(8,128)S(1)} async-done(((f32[8,48,128]{2,1,0:T(8,128)}), f32[8,48,128]{2,1,0:T(8,128)S(1)}, u32[]{:S(2)}, u32[]{:S(2)}) %all-to-all-start.3) | async-done | bytes 196640 | tf_op jit(solution)/shard_map/all_to_all | solution.py:162
  68.2 0.7 copy-done.5
  68.8 3.0 %shard_map.99 = (f32[16,64,1]{2,1,0:T(8,128)}, f32[16,64,1]{2,1,0:T(8,128)}) custom-call(s32[16]{0:T(128)} %reshape.92.refs_2_.out_idx_ref, f32[16,64,48]{2,1,0:T(8,128)} %shard_map.96.refs_3_.value_ref, f32[16,64,48]{2,1,0:T(8,128)} %bitcast.38, f32[16,64,48]{2,1,0:T(8,128)} %broadcast_in_dim.10.refs_6_.refs_5_.scale_ref, ...), custom_call_target="tpu_custom_call" | custom-call | tf_op jit(solution)/shard_map/pallas_call | solution.py:179
  71.8 1.5 %multiply_reduce_fusion = (f32[16,64]{1,0:T(8,128)S(1)}, f32[16,64]{1,0:T(8,128)S(1)}) fusion(f32[16,64,1]{2,1,0:T(8,128)} %get-tuple-element.17, f32[16,64,1]{2,1,0:T(8,128)} %get-tuple-element.16), kind=kLoop, calls=%fused_computation.1 | loop fusion | flops 3072 | bytes 16384 | tf_op jit(solution)/shard_map/div | solution.py:182
  73.6 1.6 %collective-permute-start = (f32[256,2]{0,1:T(2,128)S(1)}, f32[256,2]{0,1:T(2,128)S(1)}, u32[]{:S(2)}, u32[]{:S(2)}) collective-permute-start(f32[256,2]{0,1:T(2,128)S(1)} %bitcast.44), channel_id=1, source_target_pairs={{0,1},{1,2},{2,3},{3,0},{4,5},{5,6},{6,7},{7,4},{8,9},{9,10},{10,1... | collective-permute-start | bytes 6152 | tf_op jit(solution)/shard_map/ppermute | solution.py:190
  75.2 2.6 %collective-permute-start.1 = (f32[256,2]{0,1:T(2,128)S(1)}, f32[256,2]{0,1:T(2,128)S(1)}, u32[]{:S(2)}, u32[]{:S(2)}) collective-permute-start(f32[256,2]{0,1:T(2,128)S(1)} %bitcast.45), channel_id=1, source_target_pairs={{0,2},{1,3},{2,0},{3,1},{4,6},{5,7},{6,4},{7,5},{8,10},{9,11},{10,... | collective-permute-start | bytes 6152 | tf_op jit(solution)/shard_map/ppermute | solution.py:190
  77.8 1.3 %collective-permute-start.2 = (f32[256,2]{0,1:T(2,128)S(1)}, f32[256,2]{0,1:T(2,128)S(1)}, u32[]{:S(2)}, u32[]{:S(2)}) collective-permute-start(f32[256,2]{0,1:T(2,128)S(1)} %bitcast.46), channel_id=1, source_target_pairs={{0,3},{1,0},{2,1},{3,2},{4,7},{5,4},{6,5},{7,6},{8,11},{9,8},{10,9... | collective-permute-start | bytes 6152 | tf_op jit(solution)/shard_map/ppermute | solution.py:190
  79.1 0.5 collective-permute-done.1
  79.7 1.7 %collective-permute-done.2 = f32[256,2]{0,1:T(2,128)S(1)} collective-permute-done((f32[256,2]{0,1:T(2,128)S(1)}, f32[256,2]{0,1:T(2,128)S(1)}, u32[]{:S(2)}, u32[]{:S(2)}) %collective-permute-start.2) | collective-permute-done | bytes 2080 | tf_op jit(solution)/shard_map/ppermute | solution.py:190
  81.4 0.6 fusion.3
  (36 shorter events, 1.2 us)
Async XLA Ops:
  0.6 0.7 copy-start
  0.6 10.9 %copy-start.6 = (f32[48,1024]{1,0:T(8,128)S(1)}, f32[48,1024]{1,0:T(8,128)}, u32[]{:S(2)}) copy-start(f32[48,1024]{1,0:T(8,128)} %param.10) | copy-start | bytes 589828
  0.7 10.2 %copy-start.8 = (s32[16,8]{0,1:T(8,128)S(1)}, s32[16,8]{0,1:T(8,128)}, u32[]{:S(2)}) copy-start(s32[16,8]{0,1:T(8,128)} %param.14) | copy-start | bytes 1540
  0.7 11.9 %copy-start.7 = (f32[48,1024]{1,0:T(8,128)S(1)}, f32[48,1024]{1,0:T(8,128)}, u32[]{:S(2)}) copy-start(f32[48,1024]{1,0:T(8,128)} %param.11) | copy-start | bytes 589828
  0.7 12.1 %copy-start.1 = (f32[16,64,512]{2,1,0:T(8,128)S(1)}, f32[16,64,512]{2,1,0:T(8,128)}, u32[]{:S(2)}) copy-start(f32[16,64,512]{2,1,0:T(8,128)} %refs_5_.3) | copy-start | bytes 6291460
  5.0 11.4 %all-to-all-start = ((f32[8,48,128]{2,1,0:T(8,128)}), f32[8,48,128]{2,1,0:T(8,128)S(1)}, u32[]{:S(2)}, u32[]{:S(2)}) async-start(f32[8,48,128]{2,1,0:T(8,128)} %bitcast.28), calls=%async_computation | async-start | bytes 393216 | tf_op jit(solution)/shard_map/all_to_all | solution.py:162
  12.7 12.6 %copy-start.2 = (f32[48,1024]{0,1:T(8,128)}, f32[48,1024]{0,1:T(8,128)S(1)}, u32[]{:S(2)}) copy-start(f32[48,1024]{0,1:T(8,128)S(1)} %copy.38) | copy-start | bytes 589828
  16.4 1.0 %copy-start.3 = (f32[8,48,128]{2,1,0:T(8,128)}, f32[8,48,128]{2,1,0:T(8,128)S(1)}, u32[]{:S(2)}) copy-start(f32[8,48,128]{2,1,0:T(8,128)S(1)} %all-to-all-done.refs_4_) | copy-start | bytes 589828
  22.0 9.5 %all-to-all-start.1 = ((f32[8,48,128]{2,1,0:T(8,128)}), f32[8,48,128]{2,1,0:T(8,128)S(1)}, u32[]{:S(2)}, u32[]{:S(2)}) async-start(f32[8,48,128]{2,1,0:T(8,128)} %get-tuple-element.11), calls=%async_computation.1 | async-start | bytes 393216 | tf_op jit(solution)/shard_map/all_to_all | solution.py:162
  31.5 0.7 copy-start.4
  58.6 9.5 %all-to-all-start.3 = ((f32[8,48,128]{2,1,0:T(8,128)}), f32[8,48,128]{2,1,0:T(8,128)S(1)}, u32[]{:S(2)}, u32[]{:S(2)}) async-start(f32[8,48,128]{2,1,0:T(8,128)} %get-tuple-element.15), calls=%async_computation.3 | async-start | bytes 393216 | tf_op jit(solution)/shard_map/all_to_all | solution.py:162
  68.2 0.7 copy-start.5
  73.6 5.6 %collective-permute-start = (f32[256,2]{0,1:T(2,128)S(1)}, f32[256,2]{0,1:T(2,128)S(1)}, u32[]{:S(2)}, u32[]{:S(2)}) collective-permute-start(f32[256,2]{0,1:T(2,128)S(1)} %bitcast.44), channel_id=1, source_target_pairs={{0,1},{1,2},{2,3},{3,0},{4,5},{5,6},{6,7},{7,4},{8,9},{9,10},{10,1... | collective-permute-start | bytes 6152 | tf_op jit(solution)/shard_map/ppermute | solution.py:190
  75.2 4.5 %collective-permute-start.1 = (f32[256,2]{0,1:T(2,128)S(1)}, f32[256,2]{0,1:T(2,128)S(1)}, u32[]{:S(2)}, u32[]{:S(2)}) collective-permute-start(f32[256,2]{0,1:T(2,128)S(1)} %bitcast.45), channel_id=1, source_target_pairs={{0,2},{1,3},{2,0},{3,1},{4,6},{5,7},{6,4},{7,5},{8,10},{9,11},{10,... | collective-permute-start | bytes 6152 | tf_op jit(solution)/shard_map/ppermute | solution.py:190
  77.8 3.6 %collective-permute-start.2 = (f32[256,2]{0,1:T(2,128)S(1)}, f32[256,2]{0,1:T(2,128)S(1)}, u32[]{:S(2)}, u32[]{:S(2)}) collective-permute-start(f32[256,2]{0,1:T(2,128)S(1)} %bitcast.46), channel_id=1, source_target_pairs={{0,3},{1,0},{2,1},{3,2},{4,7},{5,4},{6,5},{7,6},{8,11},{9,8},{10,9... | collective-permute-start | bytes 6152 | tf_op jit(solution)/shard_map/ppermute | solution.py:190

commit v4 on v3

--- a/solution.py
+++ b/solution.py
@@ -23,7 +23,23 @@
     def one(u, v):
         return jnp.dot(u, v, preferred_element_type=jnp.float32)
 
-    return one(a_high, b_high) + one(a_low, b_high) + one(a_high, b_low)
+    lhs = jnp.concatenate([a_high, a_low, a_high], axis=1)
+    rhs = jnp.concatenate([b_high, b_high, b_low], axis=0)
+    return one(lhs, rhs)
+
+
+def dest_sum(x):
+    ones = jnp.ones((8, x.shape[1]), jnp.bfloat16)
+    high = x.astype(jnp.bfloat16)
+    rest = x - high.astype(jnp.float32)
+    mid = rest.astype(jnp.bfloat16)
+    low = (rest - mid.astype(jnp.float32)).astype(jnp.bfloat16)
+    dims = (((1,), (1,)), ((), ()))
+    total = sum(
+        lax.dot_general(ones, part, dims, preferred_element_type=jnp.float32)
+        for part in (high, mid, low)
+    )
+    return total[0:1]
 
 
 def live_factor(cnt_ref, n, s):
@@ -34,7 +50,7 @@
     block_len = owned.shape[1]
     capacity = out_idx_ref.shape[0] // returned_ref.shape[0]
     for p in range(returned_ref.shape[0]):
-        got = returned_ref[p].T
+        got = returned_ref[p][0 : owned.shape[2]].T
         for c in range(capacity):
             b = out_idx_ref[p * capacity + c]
             owned[b] = owned[b] + got[c * block_len : (c + 1) * block_len, :]
@@ -96,6 +112,40 @@
         ghost_out[p] = part.reshape(capacity * block_len, -1).T
 
 
+def last_kernel(cnt_ref, col_ref, out_idx_ref, value_ref, demand_ref, scale_ref, own_ref,
+                returned_ref, turn_ref, weight_ref, sums_out, ratio, totals):
+    blocks = value_ref.shape[0]
+    ghosts = out_idx_ref.shape[0]
+    slots = col_ref.shape[1]
+    block_len = value_ref.shape[1]
+    columns = value_ref.shape[2]
+    capacity = ghosts // returned_ref.shape[0]
+    totals[0:blocks] = own_ref[...]
+    add_returned(totals, out_idx_ref, returned_ref)
+    value = value_ref[...]
+    load = value * (totals[0:blocks] * scale_ref[...]) + demand_ref[...]
+    ratio[...] = load / value
+    totals[...] = jnp.zeros(totals.shape, totals.dtype)
+    for n in range(blocks):
+        terms = dot3(turn_ref[n], ratio[n])
+        for s in range(slots):
+            b = col_ref[n, s]
+            piece = terms[s * block_len : (s + 1) * block_len, :] * live_factor(cnt_ref, n, s)
+            totals[b] = totals[b] + piece
+    weight = weight_ref[...]
+    for b in range(blocks):
+        product = value_ref[b] * scale_ref[b] * totals[b]
+        sums_out[0, b : b + 1, :] = dest_sum(product + demand_ref[b])
+        sums_out[1, b : b + 1, :] = dest_sum(weight * product)
+    for p in range(returned_ref.shape[0]):
+        weighted = returned_ref[p][columns : 2 * columns].T
+        for c in range(capacity):
+            k = p * capacity + c
+            product = weighted[c * block_len : (c + 1) * block_len, :] * totals[blocks + k]
+            sums_out[0, blocks + k : blocks + k + 1, :] = dest_sum(product)
+            sums_out[1, blocks + k : blocks + k + 1, :] = dest_sum(weight * product)
+
+
 def final_kernel(out_idx_ref, value_ref, demand_ref, scale_ref, own_ref, returned_ref, weight_ref,
                  flow_out, grad_out, owned):
     owned[...] = own_ref[...]
@@ -170,25 +220,28 @@
     )
     value, send = forward(True)(*idx, exit_t, received, turn_weight, scale, exit_t)
     received = exchange(send)
-    (value,) = forward(False)(*idx, value, received, turn_weight, scale, exit_t)
+    value, send = forward(True)(*idx, value, received, turn_weight, scale, exit_t)
     own, ghost = adjoint(True)(*idx, value, demand_t, scale, demand_t, demand_t[:1], turn_t)
-    returned = exchange(ghost)
-    own, ghost = adjoint(False)(*idx, value, demand_t, scale, own, returned, turn_t)
-    returned = exchange(ghost)
-    weight = dest_weight.reshape(1, 1, columns)
-    flow_sum, grad_sum = final(outbound, value, demand_t, scale, own, returned, weight)
-    dest_total = columns * lax.axis_size("dest")
-    flow_part = flow_sum.reshape(own_len) / dest_total
-    grad_part = -grad_sum.reshape(own_len) / dest_total
-    stacked = jnp.stack([flow_part, grad_part], axis=1)
+    returned = exchange(jnp.concatenate([ghost, send], axis=1))
+    weight = dest_weight.reshape(1, columns)
+    last = pl.pallas_call(
+        last_kernel,
+        out_shape=jax.ShapeDtypeStruct((2, blocks + ghosts, block_len), f32),
+        in_specs=[smem, smem, smem] + [vmem] * 7,
+        out_specs=vmem,
+        scratch_shapes=[pltpu.VMEM(block_shape, f32), scratch],
+    )
+    sums = last(*idx, value, demand_t, scale, own, returned, turn_t, weight)
     dest_n = lax.axis_size("dest")
-    me = lax.axis_index("dest")
-    parts = stacked.reshape(dest_n, -1, 2)
-    both = lax.dynamic_index_in_dim(parts, me, 0, keepdims=False)
-    for shift in range(1, dest_n):
-        send_part = lax.dynamic_index_in_dim(parts, (me + shift) % dest_n, 0, keepdims=False)
-        both = both + lax.ppermute(send_part, "dest", shift_pairs(dest_n, shift))
-    return (both[:, 0], both[:, 1])
+    ghost_part = jnp.arange(ghosts, dtype=jnp.int32) // capacity
+    ghost_block = send_blocks[ghost_part, my_part, jnp.arange(ghosts, dtype=jnp.int32) % capacity]
+    routed = jnp.zeros((partitions, blocks, 2, block_len), f32)
+    routed = lax.dynamic_update_index_in_dim(routed, sums[:, :blocks].transpose(1, 0, 2), my_part, 0)
+    routed = routed.at[ghost_part, ghost_block].add(sums[:, blocks:].transpose(1, 0, 2))
+    routed = routed.reshape(partitions * dest_n, blocks // dest_n, 2, block_len)
+    got = lax.all_to_all(routed, ("dom", "dest"), split_axis=0, concat_axis=0, tiled=True)
+    total = jnp.sum(got, axis=0) / (columns * dest_n)
+    return (total[:, 0].reshape(-1), -total[:, 1].reshape(-1))
 
 
 def solution(mesh):

time: 82.6 us -> 80.4 us (0.973)
  starting transfers between devices: 17.5 us -> 12 us
  local copies, waits for them, and re-layouts: 11.6 us -> 14.5 us
  other arithmetic: 3.21 us -> 5.59 us
  Pallas kernels: 23.8 us -> 21.6 us
  blocking collectives: 10.2 us -> 11.3 us
    ppermute x3 -> x0, starting transfers between devices: 5.56 us -> none  [local(): both = both + lax.ppermute(send_part, 'dest', shift_pairs(dest_n, shift))]
    ppermute x3 -> x0, waiting for transfers between devices: 2.24 us -> none  [local(): both = both + lax.ppermute(send_part, 'dest', shift_pairs(dest_n, shift))]
    pallas_call x3 -> x2, Pallas kernels: 13.5 us -> 11.6 us  [the longest x1 6.94 us: local(): sums = last(*idx, value, demand_t, scale, own, returned, turn_t, weight)]
    concatenate x0 -> x3, other arithmetic: none -> 1.73 us  [the longest x1 1.7 us: local(): returned = exchange(jnp.concatenate([ghost, send], axis=1))]
    div x1, other arithmetic: 1.54 us -> 0.01 us  [local(): total = jnp.sum(got, axis=0) / (columns * dest_n)]
    all_to_all x3, waiting for transfers between devices: 12.5 us -> 14 us  [exchange(): lax.all_to_all(pieces, 'dom', split_axis=0, concat_axis=0, tiled=True)]
    scatter-add x0 -> x1, other arithmetic: none -> 1.29 us  [local(): routed.at[ghost_part, ghost_block].add(sums[:, blocks:].transpose(1, 0, 2))]
    all_to_all x1, blocking collectives: 10.2 us -> 11.3 us  [local(): lax.all_to_all(routed, ('dom', 'dest'), split_axis=0, concat_axis=0, tile...]
  transfers between devices with their start and end apart: 6 -> 3, of which waited for: 5 -> 3; matrix products, arithmetic and copies ran while one was open for 7% -> 8% of each run, Pallas kernels for 0% -> 0%
where the time goes in v4:
time: 80.4 us; the launch traced here: 79.8 us
  Pallas kernels  21.6 us (27%)
  local copies, waits for them, and re-layouts  14.5 us (18%)
  waiting for transfers between devices  14 us (17%)
  starting transfers between devices  12 us (15%)
  blocking collectives  11.3 us (14%)
  other arithmetic  5.59 us (7%)
  between operations  0.83 us (1%)
    all_to_all x3, waiting for transfers between devices, exchange(): lax.all_to_all(pieces, 'dom', split_axis=0, concat_axis=0, tiled=True)  14 us
    all_to_all x3, starting transfers between devices, exchange(): lax.all_to_all(pieces, 'dom', split_axis=0, concat_axis=0, tiled=True)  12 us
    all_to_all x1, blocking collectives, local(): lax.all_to_all(routed, ('dom', 'dest'), split_axis=0, concat_axis=0, tile...  11.3 us
    pallas_call x1, Pallas kernels, local(): sums = last(*idx, value, demand_t, scale, own, returned, turn_t, weight)  6.94 us
    unnamed x25, local copies, waits for them, and re-layouts  5.95 us
    pallas_call x1, Pallas kernels, local(): adjoint(True)(*idx, value, demand_t, scale, demand_t, demand_t[:1], turn_t)  5.32 us
    pallas_call x1, Pallas kernels, local(): forward(True)(*idx, exit_t, received, turn_weight, scale, exit_t)  4.69 us
    pallas_call x1, Pallas kernels, local(): forward(True)(*idx, value, received, turn_weight, scale, exit_t)  4.66 us
  transfers between devices with their start and end apart: 3, of which 3 were waited for; matrix products, arithmetic and copies ran while one was open for 8% of the time, Pallas kernels for 0%

profile of v4, /device:TPU:0, one launch (start us, length us, event | category | flops | bytes accessed | tf_op | source)
XLA Modules:
  0.0 79.8 jit_solution(7853893435495641956)
XLA Ops:
  0.7 0.6 copy-done
  1.5 0.7 negate_exponential_fusion
  2.2 0.9 %broadcast_multiply_fusion = f32[48,1024]{1,0:T(8,128)S(1)} fusion(f32[48,1024]{1,0:T(8,128)} %param.10, f32[1024]{0:T(1024)S(1)} %negate_exponential_fusion), kind=kLoop, calls=%fused_computation.5 | loop fusion | flops 49152 | bytes 397312 | tf_op jit(solution)/shard_map/mul | solution.py:217
  3.4 0.6 gather_fusion
  4.3 0.7 copy.50
  5.0 5.2 %all-to-all-start = ((f32[8,48,128]{2,1,0:T(8,128)}), f32[8,48,128]{2,1,0:T(8,128)S(1)}, u32[]{:S(2)}, u32[]{:S(2)}) async-start(f32[8,48,128]{2,1,0:T(8,128)} %bitcast.29), calls=%async_computation | async-start | bytes 393216 | tf_op jit(solution)/shard_map/all_to_all | solution.py:212
  10.2 0.6 reshape.142.refs_2_.out_idx_ref
  10.9 0.7 copy.45.refs_1_.col_ref
  11.5 1.0 %copy.35 = f32[1024,48]{1,0:T(8,128)} copy(f32[1024,48]{0,1:T(8,128)S(1)} %bitcast.40) | data formatting | bytes 393216 | tf_op jit(solution)/shard_map/transpose | solution.py:214
  12.7 2.7 %copy.43 = f32[16,64,512]{1,2,0:T(8,128)} copy(f32[16,64,512]{2,1,0:T(8,128)S(1)} %copy-done.1) | data formatting | bytes 4194304 | tf_op args[1]
  15.5 0.9 %all-to-all-done.refs_4_ = f32[8,48,128]{2,1,0:T(8,128)S(1)} async-done(((f32[8,48,128]{2,1,0:T(8,128)}), f32[8,48,128]{2,1,0:T(8,128)S(1)}, u32[]{:S(2)}, u32[]{:S(2)}) %all-to-all-start) | async-done | bytes 196640 | tf_op jit(solution)/shard_map/all_to_all | solution.py:212
  16.4 1.0 %broadcast_in_dim.25.refs_6_.refs_5_.scale_ref = f32[16,64,48]{2,1,0:T(8,128)} broadcast(f32[16,64]{1,0:T(8,128)S(1)} %broadcast_in_dim.24), dimensions={0,1} | broadcast | bytes 200704 | tf_op jit(solution)/shard_map/broadcast_in_dim | solution.py:173
  17.4 4.7 %shard_map.95 = (f32[16,64,48]{2,1,0:T(8,128)}, f32[8,48,128]{2,1,0:T(8,128)}) custom-call(s32[16]{0:T(128)} %cnt_ref.1, s32[16,8]{1,0:T(8,128)} %copy.45.refs_1_.col_ref, s32[16]{0:T(128)} %reshape.142.refs_2_.out_idx_ref, f32[16,64,48]{2,1,0:T(8,128)} %bitcast.36, f32[8,48,128]{2,1,0:T(8,128)} %copy-done.4, f32[16,64,512]{2,1,0:T(8,128)} %refs_5_.3, ...), custom_call_target="tpu_custom_call" | custom-call | tf_op jit(solution)/shard_map/pallas_call | solution.py:221
  22.1 3.4 %all-to-all-start.1 = ((f32[8,48,128]{2,1,0:T(8,128)}), f32[8,48,128]{2,1,0:T(8,128)S(1)}, u32[]{:S(2)}, u32[]{:S(2)}) async-start(f32[8,48,128]{2,1,0:T(8,128)} %get-tuple-element.9), calls=%async_computation.1 | async-start | bytes 393216 | tf_op jit(solution)/shard_map/all_to_all | solution.py:212
  25.5 0.6 slice_bitcast_fusion.refs_7_
  26.1 5.5 %all-to-all-done.1.refs_4_ = f32[8,48,128]{2,1,0:T(8,128)S(1)} async-done(((f32[8,48,128]{2,1,0:T(8,128)}), f32[8,48,128]{2,1,0:T(8,128)S(1)}, u32[]{:S(2)}, u32[]{:S(2)}) %all-to-all-start.1) | async-done | bytes 196640 | tf_op jit(solution)/shard_map/all_to_all | solution.py:212
  31.6 0.7 copy-done.5
  32.3 4.7 %shard_map.96 = (f32[16,64,48]{2,1,0:T(8,128)}, f32[8,48,128]{2,1,0:T(8,128)}) custom-call(s32[16]{0:T(128)} %cnt_ref.1, s32[16,8]{1,0:T(8,128)} %copy.45.refs_1_.col_ref, s32[16]{0:T(128)} %reshape.142.refs_2_.out_idx_ref, f32[16,64,48]{2,1,0:T(8,128)} %get-tuple-element.8.refs_3_, f32[8,48,128]{2,1,0:T(8,128)} %copy-done.5, f32[16,64,512]{2,1,0:T(8,128)} %refs_5_.3, ...), custom_call_target="tpu_custom_call" | custom-call | tf_op jit(solution)/shard_map/pallas_call | solution.py:223
  37.0 5.3 %shard_map.97 = (f32[16,64,48]{2,1,0:T(8,128)}, f32[8,48,128]{2,1,0:T(8,128)}) custom-call(s32[16]{0:T(128)} %cnt_ref.1, s32[16,8]{1,0:T(8,128)} %copy.45.refs_1_.col_ref, s32[16]{0:T(128)} %reshape.142.refs_2_.out_idx_ref, f32[16,64,48]{2,1,0:T(8,128)} %get-tuple-element.10.refs_3_.value_ref, f32[16,64,48]{2,1,0:T(8,128)} %bitcast.33, ...), custom_call_target="tpu_custom_call" | custom-call | tf_op jit(solution)/shard_map/pallas_call | solution.py:224
  42.3 1.7 %pad_maximum_fusion = f32[8,96,128]{2,1,0:T(8,128)} fusion(f32[8,48,128]{2,1,0:T(8,128)S(1)} %copy-done.8, f32[8,48,128]{2,1,0:T(8,128)} %get-tuple-element.12), kind=kLoop, calls=%fused_computation.3 | loop fusion | flops 98304 | bytes 786432 | tf_op jit(solution)/shard_map/concatenate | solution.py:225
  44.0 3.5 %all-to-all-start.2 = ((f32[8,96,128]{2,1,0:T(8,128)}), f32[8,96,128]{2,1,0:T(8,128)S(1)}, u32[]{:S(2)}, u32[]{:S(2)}) async-start(f32[8,96,128]{2,1,0:T(8,128)} %pad_maximum_fusion), calls=%async_computation.2 | async-start | bytes 786432 | tf_op jit(solution)/shard_map/all_to_all | solution.py:212
  47.5 0.7 gather_fusion.1
  48.2 7.5 %all-to-all-done.2.returned_ref = f32[8,96,128]{2,1,0:T(8,128)S(1)} async-done(((f32[8,96,128]{2,1,0:T(8,128)}), f32[8,96,128]{2,1,0:T(8,128)S(1)}, u32[]{:S(2)}, u32[]{:S(2)}) %all-to-all-start.2) | async-done | bytes 393248 | tf_op jit(solution)/shard_map/all_to_all | solution.py:212
  55.7 0.7 copy-done.3
  56.4 6.9 %shard_map.98 = f32[2,32,64]{2,1,0:T(8,128)} custom-call(s32[16]{0:T(128)} %cnt_ref.1, s32[16,8]{1,0:T(8,128)} %copy.45.refs_1_.col_ref, s32[16]{0:T(128)} %reshape.142.refs_2_.out_idx_ref, f32[16,64,48]{2,1,0:T(8,128)} %get-tuple-element.10.refs_3_.value_ref, f32[16,64,48]{2,1,0:T(8,128)} %bitcast.35, ...), custom_call_target="tpu_custom_call" | custom-call | tf_op jit(solution)/shard_map/pallas_call | solution.py:234
  63.4 0.7 slice_bitcast_fusion.1
  64.2 1.3 %scatter_fusion = f32[8,16,2,64]{3,2,1,0:T(2,128)S(1)} fusion(f32[8,16,2,64]{3,2,1,0:T(2,128)S(1)} %copy_dynamic-update-slice_fusion, s32[16]{0:T(128)S(1)} %fusion.7, f32[16,2,64]{2,1,0:T(2,128)S(1)} %copy.47), kind=kCustom, calls=%fused_computation.2 | custom fusion | flops 2048 | bytes 24704 | tf_op jit(solution)/shard_map/scatter-add | solution.py:240
  65.7 11.3 %all_to_all.20 = f32[32,1,512]{2,1,0:T(1,128)S(1)} all-to-all(f32[32,1,512]{2,1,0:T(1,128)S(1)} %reshape.182), channel_id=1, replica_groups=mesh['dom'=8,'dest'=4] {'dom','dest'}, dimensions={0} | all-to-all | bytes 131072 | tf_op jit(solution)/shard_map/all_to_all | solution.py:242
  76.9 0.5 broadcast.226
  77.4 0.8 %reduce.8 = f32[32,512]{1,0:T(8,128)S(1)} reduce(f32[32,1,512]{2,1,0:T(1,128)S(1)} %all_to_all.20, f32[]{:T(128)} %broadcast.226), dimensions={1}, to_apply=%all_to_all.15.reduce_sub_computation | reduce | bytes 131076 | tf_op jit(solution)/shard_map/all_to_all | solution.py:242
  78.5 0.6 neg.12
  79.1 0.6 reshape_squeeze.4
  (37 shorter events, 1.5 us)
Async XLA Ops:
  0.6 0.7 copy-start
  0.6 10.9 %copy-start.6 = (f32[48,1024]{1,0:T(8,128)S(1)}, f32[48,1024]{1,0:T(8,128)}, u32[]{:S(2)}) copy-start(f32[48,1024]{1,0:T(8,128)} %param.10) | copy-start | bytes 589828
  0.7 10.2 %copy-start.9 = (s32[16,8]{0,1:T(8,128)S(1)}, s32[16,8]{0,1:T(8,128)}, u32[]{:S(2)}) copy-start(s32[16,8]{0,1:T(8,128)} %param.14) | copy-start | bytes 1540
  0.7 11.9 %copy-start.7 = (f32[48,1024]{1,0:T(8,128)S(1)}, f32[48,1024]{1,0:T(8,128)}, u32[]{:S(2)}) copy-start(f32[48,1024]{1,0:T(8,128)} %param.11) | copy-start | bytes 589828
  0.7 12.1 %copy-start.1 = (f32[16,64,512]{2,1,0:T(8,128)S(1)}, f32[16,64,512]{2,1,0:T(8,128)}, u32[]{:S(2)}) copy-start(f32[16,64,512]{2,1,0:T(8,128)} %refs_5_.3) | copy-start | bytes 6291460
  5.0 11.4 %all-to-all-start = ((f32[8,48,128]{2,1,0:T(8,128)}), f32[8,48,128]{2,1,0:T(8,128)S(1)}, u32[]{:S(2)}, u32[]{:S(2)}) async-start(f32[8,48,128]{2,1,0:T(8,128)} %bitcast.29), calls=%async_computation | async-start | bytes 393216 | tf_op jit(solution)/shard_map/all_to_all | solution.py:212
  12.7 12.8 %copy-start.2 = (f32[48,1024]{0,1:T(8,128)}, f32[48,1024]{0,1:T(8,128)S(1)}, u32[]{:S(2)}) copy-start(f32[48,1024]{0,1:T(8,128)S(1)} %copy.42) | copy-start | bytes 589828
  16.4 1.0 %copy-start.4 = (f32[8,48,128]{2,1,0:T(8,128)}, f32[8,48,128]{2,1,0:T(8,128)S(1)}, u32[]{:S(2)}) copy-start(f32[8,48,128]{2,1,0:T(8,128)S(1)} %all-to-all-done.refs_4_) | copy-start | bytes 589828
  22.1 9.5 %all-to-all-start.1 = ((f32[8,48,128]{2,1,0:T(8,128)}), f32[8,48,128]{2,1,0:T(8,128)S(1)}, u32[]{:S(2)}, u32[]{:S(2)}) async-start(f32[8,48,128]{2,1,0:T(8,128)} %get-tuple-element.9), calls=%async_computation.1 | async-start | bytes 393216 | tf_op jit(solution)/shard_map/all_to_all | solution.py:212
  31.6 0.7 copy-start.5
  37.0 5.3 %copy-start.8 = (f32[8,48,128]{2,1,0:T(8,128)S(1)}, f32[8,48,128]{2,1,0:T(8,128)}, u32[]{:S(2)}) copy-start(f32[8,48,128]{2,1,0:T(8,128)} %get-tuple-element.13) | copy-start | bytes 589828
  44.0 11.7 %all-to-all-start.2 = ((f32[8,96,128]{2,1,0:T(8,128)}), f32[8,96,128]{2,1,0:T(8,128)S(1)}, u32[]{:S(2)}, u32[]{:S(2)}) async-start(f32[8,96,128]{2,1,0:T(8,128)} %pad_maximum_fusion), calls=%async_computation.2 | async-start | bytes 786432 | tf_op jit(solution)/shard_map/all_to_all | solution.py:212
  55.7 0.7 copy-start.3

commit v5 on v4

--- a/solution.py
+++ b/solution.py
@@ -85,7 +85,7 @@
 
 
 def adjoint_kernel(first, cnt_ref, col_ref, out_idx_ref, value_ref, demand_ref, scale_ref,
-                   own_ref, returned_ref, turn_ref, own_out, ghost_out, ratio, totals):
+                   own_ref, returned_ref, turn_ref, extra_ref, own_out, ghost_out, ratio, totals):
     blocks = value_ref.shape[0]
     ghosts = out_idx_ref.shape[0]
     slots = col_ref.shape[1]
@@ -109,11 +109,12 @@
     own_out[...] = totals[0:blocks]
     for p in range(ghost_out.shape[0]):
         part = totals[blocks + p * capacity : blocks + (p + 1) * capacity]
-        ghost_out[p] = part.reshape(capacity * block_len, -1).T
-
-
-def last_kernel(cnt_ref, col_ref, out_idx_ref, value_ref, demand_ref, scale_ref, own_ref,
-                returned_ref, turn_ref, weight_ref, sums_out, ratio, totals):
+        ghost_out[p, 0 : value_ref.shape[2]] = part.reshape(capacity * block_len, -1).T
+        ghost_out[p, value_ref.shape[2] :] = extra_ref[p]
+
+
+def last_kernel(cnt_ref, col_ref, out_idx_ref, place_ref, value_ref, demand_ref, scale_ref, own_ref,
+                returned_ref, turn_ref, weight_ref, routed_out, ratio, totals):
     blocks = value_ref.shape[0]
     ghosts = out_idx_ref.shape[0]
     slots = col_ref.shape[1]
@@ -133,17 +134,20 @@
             piece = terms[s * block_len : (s + 1) * block_len, :] * live_factor(cnt_ref, n, s)
             totals[b] = totals[b] + piece
     weight = weight_ref[...]
+    routed_out[...] = jnp.zeros(routed_out.shape, routed_out.dtype)
+    me = place_ref[0]
     for b in range(blocks):
         product = value_ref[b] * scale_ref[b] * totals[b]
-        sums_out[0, b : b + 1, :] = dest_sum(product + demand_ref[b])
-        sums_out[1, b : b + 1, :] = dest_sum(weight * product)
+        routed_out[me, b, 0:1, :] = dest_sum(product + demand_ref[b])
+        routed_out[me, b, 1:2, :] = dest_sum(weight * product)
     for p in range(returned_ref.shape[0]):
         weighted = returned_ref[p][columns : 2 * columns].T
         for c in range(capacity):
             k = p * capacity + c
+            blk = place_ref[1 + k]
             product = weighted[c * block_len : (c + 1) * block_len, :] * totals[blocks + k]
-            sums_out[0, blocks + k : blocks + k + 1, :] = dest_sum(product)
-            sums_out[1, blocks + k : blocks + k + 1, :] = dest_sum(weight * product)
+            routed_out[p, blk, 0:1, :] = routed_out[p, blk, 0:1, :] + dest_sum(product)
+            routed_out[p, blk, 1:2, :] = routed_out[p, blk, 1:2, :] + dest_sum(weight * product)
 
 
 def final_kernel(out_idx_ref, value_ref, demand_ref, scale_ref, own_ref, returned_ref, weight_ref,
@@ -189,10 +193,11 @@
         )
 
     def adjoint(first):
+        doubled = (partitions, 2 * columns, capacity * block_len)
         return pl.pallas_call(
             lambda *refs: adjoint_kernel(first, *refs),
-            out_shape=(jax.ShapeDtypeStruct(block_shape, f32), jax.ShapeDtypeStruct(ghost_shape, f32)),
-            in_specs=[smem, smem, smem] + [vmem] * 6,
+            out_shape=(jax.ShapeDtypeStruct(block_shape, f32), jax.ShapeDtypeStruct(doubled, f32)),
+            in_specs=[smem, smem, smem] + [vmem] * 7,
             out_specs=(vmem, vmem),
             scratch_shapes=[pltpu.VMEM(block_shape, f32), scratch],
         )
@@ -221,23 +226,21 @@
     value, send = forward(True)(*idx, exit_t, received, turn_weight, scale, exit_t)
     received = exchange(send)
     value, send = forward(True)(*idx, value, received, turn_weight, scale, exit_t)
-    own, ghost = adjoint(True)(*idx, value, demand_t, scale, demand_t, demand_t[:1], turn_t)
-    returned = exchange(jnp.concatenate([ghost, send], axis=1))
+    own, ghost = adjoint(True)(*idx, value, demand_t, scale, demand_t, demand_t[:1], turn_t, send)
+    returned = exchange(ghost)
     weight = dest_weight.reshape(1, columns)
+    ghost_part = jnp.arange(ghosts, dtype=jnp.int32) // capacity
+    ghost_block = send_blocks[ghost_part, my_part, jnp.arange(ghosts, dtype=jnp.int32) % capacity]
+    place = jnp.concatenate([my_part.astype(jnp.int32).reshape(1), ghost_block.astype(jnp.int32)])
     last = pl.pallas_call(
         last_kernel,
-        out_shape=jax.ShapeDtypeStruct((2, blocks + ghosts, block_len), f32),
-        in_specs=[smem, smem, smem] + [vmem] * 7,
+        out_shape=jax.ShapeDtypeStruct((partitions, blocks, 2, block_len), f32),
+        in_specs=[smem, smem, smem, smem] + [vmem] * 7,
         out_specs=vmem,
         scratch_shapes=[pltpu.VMEM(block_shape, f32), scratch],
     )
-    sums = last(*idx, value, demand_t, scale, own, returned, turn_t, weight)
+    routed = last(*idx, place, value, demand_t, scale, own, returned, turn_t, weight)
     dest_n = lax.axis_size("dest")
-    ghost_part = jnp.arange(ghosts, dtype=jnp.int32) // capacity
-    ghost_block = send_blocks[ghost_part, my_part, jnp.arange(ghosts, dtype=jnp.int32) % capacity]
-    routed = jnp.zeros((partitions, blocks, 2, block_len), f32)
-    routed = lax.dynamic_update_index_in_dim(routed, sums[:, :blocks].transpose(1, 0, 2), my_part, 0)
-    routed = routed.at[ghost_part, ghost_block].add(sums[:, blocks:].transpose(1, 0, 2))
     routed = routed.reshape(partitions * dest_n, blocks // dest_n, 2, block_len)
     got = lax.all_to_all(routed, ("dom", "dest"), split_axis=0, concat_axis=0, tiled=True)
     total = jnp.sum(got, axis=0) / (columns * dest_n)

time: 80.4 us -> 77.4 us (0.963)
  other arithmetic: 5.59 us -> 3.26 us
    scatter-add x1 -> x0, other arithmetic: 1.29 us -> none  [local(): routed.at[ghost_part, ghost_block].add(sums[:, blocks:].transpose(1, 0, 2))]
    concatenate x2 -> x1, other arithmetic: 1.71 us -> 0.61 us  [local(): jnp.concatenate([my_part.astype(jnp.int32).reshape(1), ghost_block.astype...]
    unnamed x25 -> x23, local copies, waits for them, and re-layouts: 5.95 us -> 6.85 us
  transfers between devices with their start and end apart: 3 -> 3, of which waited for: 3 -> 3; matrix products, arithmetic and copies ran while one was open for 8% -> 9% of each run, Pallas kernels for 0% -> 0%
where the time goes in v5:
time: 77.4 us; the launch traced here: 76.9 us
  Pallas kernels  21.6 us (28%)
  local copies, waits for them, and re-layouts  14.6 us (19%)
  waiting for transfers between devices  13.4 us (17%)
  starting transfers between devices  12 us (16%)
  blocking collectives  11.3 us (15%)
  other arithmetic  3.26 us (4%)
  between operations  0.8 us (1%)
    all_to_all x3, waiting for transfers between devices, exchange(): lax.all_to_all(pieces, 'dom', split_axis=0, concat_axis=0, tiled=True)  13.4 us
    all_to_all x3, starting transfers between devices, exchange(): lax.all_to_all(pieces, 'dom', split_axis=0, concat_axis=0, tiled=True)  12 us
    all_to_all x1, blocking collectives, local(): lax.all_to_all(routed, ('dom', 'dest'), split_axis=0, concat_axis=0, tile...  11.3 us
    pallas_call x1, Pallas kernels, local(): last(*idx, place, value, demand_t, scale, own, returned, turn_t, weight)  6.99 us
    unnamed x23, local copies, waits for them, and re-layouts  6.85 us
    pallas_call x1, Pallas kernels, local(): adjoint(True)  5.29 us
    pallas_call x1, Pallas kernels, local(): forward(True)(*idx, exit_t, received, turn_weight, scale, exit_t)  4.69 us
    pallas_call x1, Pallas kernels, local(): forward(True)(*idx, value, received, turn_weight, scale, exit_t)  4.66 us
  transfers between devices with their start and end apart: 3, of which 3 were waited for; matrix products, arithmetic and copies ran while one was open for 9% of the time, Pallas kernels for 0%

profile of v5, /device:TPU:0, one launch (start us, length us, event | category | flops | bytes accessed | tf_op | source)
XLA Modules:
  0.0 76.9 jit_solution(6890574678958578527)
XLA Ops:
  0.7 0.6 copy-done
  1.4 0.8 negate_exponential_fusion
  2.2 0.9 %broadcast_multiply_fusion = f32[48,1024]{1,0:T(8,128)S(1)} fusion(f32[48,1024]{1,0:T(8,128)} %param.10, f32[1024]{0:T(1024)S(1)} %negate_exponential_fusion), kind=kLoop, calls=%fused_computation.3 | loop fusion | flops 49152 | bytes 397312 | tf_op jit(solution)/shard_map/mul | solution.py:222
  3.5 0.6 gather_fusion.1
  4.3 0.7 copy.43
  5.0 5.2 %all-to-all-start = ((f32[8,48,128]{2,1,0:T(8,128)}), f32[8,48,128]{2,1,0:T(8,128)S(1)}, u32[]{:S(2)}, u32[]{:S(2)}) async-start(f32[8,48,128]{2,1,0:T(8,128)} %bitcast.18), calls=%async_computation | async-start | bytes 393216 | tf_op jit(solution)/shard_map/all_to_all | solution.py:217
  10.2 0.6 reshape.132.refs_2_.out_idx_ref
  10.9 0.7 copy.41.refs_1_.col_ref
  11.6 1.0 %copy.31 = f32[1024,48]{1,0:T(8,128)} copy(f32[1024,48]{0,1:T(8,128)S(1)} %bitcast.29) | data formatting | bytes 393216 | tf_op jit(solution)/shard_map/transpose | solution.py:219
  12.6 0.2 copy.38
  12.8 2.7 %copy.39 = f32[16,64,512]{1,2,0:T(8,128)} copy(f32[16,64,512]{2,1,0:T(8,128)S(1)} %copy-done.1) | data formatting | bytes 4194304 | tf_op args[1]
  15.5 0.9 %all-to-all-done.refs_4_ = f32[8,48,128]{2,1,0:T(8,128)S(1)} async-done(((f32[8,48,128]{2,1,0:T(8,128)}), f32[8,48,128]{2,1,0:T(8,128)S(1)}, u32[]{:S(2)}, u32[]{:S(2)}) %all-to-all-start) | async-done | bytes 196640 | tf_op jit(solution)/shard_map/all_to_all | solution.py:217
  16.4 1.0 %broadcast_in_dim.16.refs_6_.refs_5_.scale_ref = f32[16,64,48]{2,1,0:T(8,128)} broadcast(f32[16,64]{1,0:T(8,128)S(1)} %broadcast_in_dim.7), dimensions={0,1} | broadcast | bytes 200704 | tf_op jit(solution)/shard_map/broadcast_in_dim | solution.py:177
  17.4 4.7 %shard_map.95 = (f32[16,64,48]{2,1,0:T(8,128)}, f32[8,48,128]{2,1,0:T(8,128)}) custom-call(s32[16]{0:T(128)} %cnt_ref.1, s32[16,8]{1,0:T(8,128)} %copy.41.refs_1_.col_ref, s32[16]{0:T(128)} %reshape.132.refs_2_.out_idx_ref, f32[16,64,48]{2,1,0:T(8,128)} %bitcast.25, f32[8,48,128]{2,1,0:T(8,128)} %copy-done.4, f32[16,64,512]{2,1,0:T(8,128)} %refs_5_.3, ...), custom_call_target="tpu_custom_call" | custom-call | tf_op jit(solution)/shard_map/pallas_call | solution.py:226
  22.1 3.4 %all-to-all-start.1 = ((f32[8,48,128]{2,1,0:T(8,128)}), f32[8,48,128]{2,1,0:T(8,128)S(1)}, u32[]{:S(2)}, u32[]{:S(2)}) async-start(f32[8,48,128]{2,1,0:T(8,128)} %get-tuple-element.9), calls=%async_computation.1 | async-start | bytes 393216 | tf_op jit(solution)/shard_map/all_to_all | solution.py:217
  25.5 0.6 slice_bitcast_fusion.refs_7_
  26.1 5.5 %all-to-all-done.1.refs_4_ = f32[8,48,128]{2,1,0:T(8,128)S(1)} async-done(((f32[8,48,128]{2,1,0:T(8,128)}), f32[8,48,128]{2,1,0:T(8,128)S(1)}, u32[]{:S(2)}, u32[]{:S(2)}) %all-to-all-start.1) | async-done | bytes 196640 | tf_op jit(solution)/shard_map/all_to_all | solution.py:217
  31.7 0.7 copy-done.5
  32.4 4.7 %shard_map.96 = (f32[16,64,48]{2,1,0:T(8,128)}, f32[8,48,128]{2,1,0:T(8,128)}) custom-call(s32[16]{0:T(128)} %cnt_ref.1, s32[16,8]{1,0:T(8,128)} %copy.41.refs_1_.col_ref, s32[16]{0:T(128)} %reshape.132.refs_2_.out_idx_ref, f32[16,64,48]{2,1,0:T(8,128)} %get-tuple-element.8.refs_3_, f32[8,48,128]{2,1,0:T(8,128)} %copy-done.5, f32[16,64,512]{2,1,0:T(8,128)} %refs_5_.3, ...), custom_call_target="tpu_custom_call" | custom-call | tf_op jit(solution)/shard_map/pallas_call | solution.py:228
  37.0 5.3 %shard_map.97 = (f32[16,64,48]{2,1,0:T(8,128)}, f32[8,96,128]{2,1,0:T(8,128)}) custom-call(s32[16]{0:T(128)} %cnt_ref.1, s32[16,8]{1,0:T(8,128)} %copy.41.refs_1_.col_ref, s32[16]{0:T(128)} %reshape.132.refs_2_.out_idx_ref, f32[16,64,48]{2,1,0:T(8,128)} %get-tuple-element.10.refs_3_.value_ref, f32[16,64,48]{2,1,0:T(8,128)} %bitcast.22, ...), custom_call_target="tpu_custom_call" | custom-call | tf_op jit(solution)/shard_map/pallas_call | solution.py:229
  42.3 3.5 %all-to-all-start.2 = ((f32[8,96,128]{2,1,0:T(8,128)}), f32[8,96,128]{2,1,0:T(8,128)S(1)}, u32[]{:S(2)}, u32[]{:S(2)}) async-start(f32[8,96,128]{2,1,0:T(8,128)} %get-tuple-element.13), calls=%async_computation.2 | async-start | bytes 786432 | tf_op jit(solution)/shard_map/all_to_all | solution.py:217
  45.8 0.7 gather_fusion
  46.5 0.6 pad_add_fusion.place_ref
  47.1 6.9 %all-to-all-done.2.returned_ref = f32[8,96,128]{2,1,0:T(8,128)S(1)} async-done(((f32[8,96,128]{2,1,0:T(8,128)}), f32[8,96,128]{2,1,0:T(8,128)S(1)}, u32[]{:S(2)}, u32[]{:S(2)}) %all-to-all-start.2) | async-done | bytes 393248 | tf_op jit(solution)/shard_map/all_to_all | solution.py:217
  54.0 0.7 copy-done.3
  54.8 7.0 %shard_map.98 = f32[8,16,2,64]{3,2,1,0:T(2,128)} custom-call(s32[16]{0:T(128)} %cnt_ref.1, s32[16,8]{1,0:T(8,128)} %copy.41.refs_1_.col_ref, s32[16]{0:T(128)} %reshape.132.refs_2_.out_idx_ref, s32[17]{0:T(128)} %pad_add_fusion.place_ref, f32[16,64,48]{2,1,0:T(8,128)} %get-tuple-element.10.refs_3_.value_ref, f32[16,64,48]{2,1,0:T(8,128)} %bitcast.24, ...), custom_call_target="tpu_custom_call" | custom-call | tf_op jit(solution)/shard_map/pallas_call | solution.py:242
  61.8 1.0 %reshape.167 = f32[32,1,512]{2,1,0:T(1,128)S(1)} reshape(f32[32,4,2,64]{3,2,1,0:T(2,128)} %bitcast.30) | data formatting | bytes 131072
  62.8 11.3 %all_to_all.20 = f32[32,1,512]{2,1,0:T(1,128)S(1)} all-to-all(f32[32,1,512]{2,1,0:T(1,128)S(1)} %reshape.167), channel_id=1, replica_groups=mesh['dom'=8,'dest'=4] {'dom','dest'}, dimensions={0} | all-to-all | bytes 131072 | tf_op jit(solution)/shard_map/all_to_all | solution.py:245
  74.1 0.5 broadcast.174
  74.6 0.8 %reduce.8 = f32[32,512]{1,0:T(8,128)S(1)} reduce(f32[32,1,512]{2,1,0:T(1,128)S(1)} %all_to_all.20, f32[]{:T(128)} %broadcast.174), dimensions={1}, to_apply=%all_to_all.15.reduce_sub_computation | reduce | bytes 131076 | tf_op jit(solution)/shard_map/all_to_all | solution.py:245
  75.6 0.6 reshape_squeeze.4
  76.3 0.6 neg.12
  (30 shorter events, 1.0 us)
Async XLA Ops:
  0.6 0.7 copy-start
  0.6 10.9 %copy-start.6 = (f32[48,1024]{1,0:T(8,128)S(1)}, f32[48,1024]{1,0:T(8,128)}, u32[]{:S(2)}) copy-start(f32[48,1024]{1,0:T(8,128)} %param.10) | copy-start | bytes 589828
  0.7 10.2 %copy-start.8 = (s32[16,8]{0,1:T(8,128)S(1)}, s32[16,8]{0,1:T(8,128)}, u32[]{:S(2)}) copy-start(s32[16,8]{0,1:T(8,128)} %param.14) | copy-start | bytes 1540
  0.7 11.9 %copy-start.7 = (f32[48,1024]{1,0:T(8,128)S(1)}, f32[48,1024]{1,0:T(8,128)}, u32[]{:S(2)}) copy-start(f32[48,1024]{1,0:T(8,128)} %param.11) | copy-start | bytes 589828
  0.7 12.1 %copy-start.1 = (f32[16,64,512]{2,1,0:T(8,128)S(1)}, f32[16,64,512]{2,1,0:T(8,128)}, u32[]{:S(2)}) copy-start(f32[16,64,512]{2,1,0:T(8,128)} %refs_5_.3) | copy-start | bytes 6291460
  5.0 11.4 %all-to-all-start = ((f32[8,48,128]{2,1,0:T(8,128)}), f32[8,48,128]{2,1,0:T(8,128)S(1)}, u32[]{:S(2)}, u32[]{:S(2)}) async-start(f32[8,48,128]{2,1,0:T(8,128)} %bitcast.18), calls=%async_computation | async-start | bytes 393216 | tf_op jit(solution)/shard_map/all_to_all | solution.py:217
  12.8 12.8 %copy-start.2 = (f32[48,1024]{0,1:T(8,128)}, f32[48,1024]{0,1:T(8,128)S(1)}, u32[]{:S(2)}) copy-start(f32[48,1024]{0,1:T(8,128)S(1)} %copy.38) | copy-start | bytes 589828
  16.4 1.0 %copy-start.4 = (f32[8,48,128]{2,1,0:T(8,128)}, f32[8,48,128]{2,1,0:T(8,128)S(1)}, u32[]{:S(2)}) copy-start(f32[8,48,128]{2,1,0:T(8,128)S(1)} %all-to-all-done.refs_4_) | copy-start | bytes 589828
  22.1 9.5 %all-to-all-start.1 = ((f32[8,48,128]{2,1,0:T(8,128)}), f32[8,48,128]{2,1,0:T(8,128)S(1)}, u32[]{:S(2)}, u32[]{:S(2)}) async-start(f32[8,48,128]{2,1,0:T(8,128)} %get-tuple-element.9), calls=%async_computation.1 | async-start | bytes 393216 | tf_op jit(solution)/shard_map/all_to_all | solution.py:217
  31.7 0.7 copy-start.5
  42.3 11.7 %all-to-all-start.2 = ((f32[8,96,128]{2,1,0:T(8,128)}), f32[8,96,128]{2,1,0:T(8,128)S(1)}, u32[]{:S(2)}, u32[]{:S(2)}) async-start(f32[8,96,128]{2,1,0:T(8,128)} %get-tuple-element.13), calls=%async_computation.2 | async-start | bytes 786432 | tf_op jit(solution)/shard_map/all_to_all | solution.py:217
  54.0 0.7 copy-start.3

commit v6 on v5

--- a/solution.py
+++ b/solution.py
@@ -30,15 +30,11 @@
 
 def dest_sum(x):
     ones = jnp.ones((8, x.shape[1]), jnp.bfloat16)
-    high = x.astype(jnp.bfloat16)
-    rest = x - high.astype(jnp.float32)
-    mid = rest.astype(jnp.bfloat16)
-    low = (rest - mid.astype(jnp.float32)).astype(jnp.bfloat16)
+    high, low = split_bf16(x)
     dims = (((1,), (1,)), ((), ()))
-    total = sum(
-        lax.dot_general(ones, part, dims, preferred_element_type=jnp.float32)
-        for part in (high, mid, low)
-    )
+    parts = jnp.concatenate([high, low], axis=0)
+    total = lax.dot_general(ones, parts, dims, preferred_element_type=jnp.float32)
+    total = total[:, 0 : x.shape[0]] + total[:, x.shape[0] :]
     return total[0:1]
 
 

time: 77.4 us -> 77 us (level)
  no operation moved by 1% of the time
where the time goes in v6:
time: 77 us; the launch traced here: 76.4 us
  Pallas kernels  21.1 us (27%)
  local copies, waits for them, and re-layouts  14.6 us (19%)
  waiting for transfers between devices  13.4 us (17%)
  starting transfers between devices  12 us (16%)
  blocking collectives  11.3 us (15%)
  other arithmetic  3.26 us (4%)
  between operations  0.8 us (1%)
    all_to_all x3, waiting for transfers between devices, exchange(): lax.all_to_all(pieces, 'dom', split_axis=0, concat_axis=0, tiled=True)  13.4 us
    all_to_all x3, starting transfers between devices, exchange(): lax.all_to_all(pieces, 'dom', split_axis=0, concat_axis=0, tiled=True)  12 us
    all_to_all x1, blocking collectives, local(): lax.all_to_all(routed, ('dom', 'dest'), split_axis=0, concat_axis=0, tile...  11.3 us
    unnamed x23, local copies, waits for them, and re-layouts  6.85 us
    pallas_call x1, Pallas kernels, local(): last(*idx, place, value, demand_t, scale, own, returned, turn_t, weight)  6.51 us
    pallas_call x1, Pallas kernels, local(): adjoint(True)  5.29 us
    pallas_call x1, Pallas kernels, local(): forward(True)(*idx, exit_t, received, turn_weight, scale, exit_t)  4.69 us
    pallas_call x1, Pallas kernels, local(): forward(True)(*idx, value, received, turn_weight, scale, exit_t)  4.66 us
  transfers between devices with their start and end apart: 3, of which 3 were waited for; matrix products, arithmetic and copies ran while one was open for 9% of the time, Pallas kernels for 0%

profile of v6, /device:TPU:0, one launch (start us, length us, event | category | flops | bytes accessed | tf_op | source)
XLA Modules:
  0.0 76.4 jit_solution(11775619080167032256)
XLA Ops:
  0.7 0.6 copy-done
  1.4 0.8 negate_exponential_fusion
  2.2 0.9 %broadcast_multiply_fusion = f32[48,1024]{1,0:T(8,128)S(1)} fusion(f32[48,1024]{1,0:T(8,128)} %param.10, f32[1024]{0:T(1024)S(1)} %negate_exponential_fusion), kind=kLoop, calls=%fused_computation.3 | loop fusion | flops 49152 | bytes 397312 | tf_op jit(solution)/shard_map/mul | solution.py:218
  3.5 0.6 gather_fusion.1
  4.3 0.7 copy.43
  5.0 5.2 %all-to-all-start = ((f32[8,48,128]{2,1,0:T(8,128)}), f32[8,48,128]{2,1,0:T(8,128)S(1)}, u32[]{:S(2)}, u32[]{:S(2)}) async-start(f32[8,48,128]{2,1,0:T(8,128)} %bitcast.18), calls=%async_computation | async-start | bytes 393216 | tf_op jit(solution)/shard_map/all_to_all | solution.py:213
  10.2 0.6 reshape.132.refs_2_.out_idx_ref
  10.9 0.7 copy.41.refs_1_.col_ref
  11.6 1.0 %copy.31 = f32[1024,48]{1,0:T(8,128)} copy(f32[1024,48]{0,1:T(8,128)S(1)} %bitcast.29) | data formatting | bytes 393216 | tf_op jit(solution)/shard_map/transpose | solution.py:215
  12.6 0.2 copy.38
  12.8 2.7 %copy.39 = f32[16,64,512]{1,2,0:T(8,128)} copy(f32[16,64,512]{2,1,0:T(8,128)S(1)} %copy-done.1) | data formatting | bytes 4194304 | tf_op args[1]
  15.5 0.9 %all-to-all-done.refs_4_ = f32[8,48,128]{2,1,0:T(8,128)S(1)} async-done(((f32[8,48,128]{2,1,0:T(8,128)}), f32[8,48,128]{2,1,0:T(8,128)S(1)}, u32[]{:S(2)}, u32[]{:S(2)}) %all-to-all-start) | async-done | bytes 196640 | tf_op jit(solution)/shard_map/all_to_all | solution.py:213
  16.4 1.0 %broadcast_in_dim.16.refs_6_.refs_5_.scale_ref = f32[16,64,48]{2,1,0:T(8,128)} broadcast(f32[16,64]{1,0:T(8,128)S(1)} %broadcast_in_dim.7), dimensions={0,1} | broadcast | bytes 200704 | tf_op jit(solution)/shard_map/broadcast_in_dim | solution.py:173
  17.4 4.7 %shard_map.95 = (f32[16,64,48]{2,1,0:T(8,128)}, f32[8,48,128]{2,1,0:T(8,128)}) custom-call(s32[16]{0:T(128)} %cnt_ref.1, s32[16,8]{1,0:T(8,128)} %copy.41.refs_1_.col_ref, s32[16]{0:T(128)} %reshape.132.refs_2_.out_idx_ref, f32[16,64,48]{2,1,0:T(8,128)} %bitcast.25, f32[8,48,128]{2,1,0:T(8,128)} %copy-done.4, f32[16,64,512]{2,1,0:T(8,128)} %refs_5_.3, ...), custom_call_target="tpu_custom_call" | custom-call | tf_op jit(solution)/shard_map/pallas_call | solution.py:222
  22.1 3.4 %all-to-all-start.1 = ((f32[8,48,128]{2,1,0:T(8,128)}), f32[8,48,128]{2,1,0:T(8,128)S(1)}, u32[]{:S(2)}, u32[]{:S(2)}) async-start(f32[8,48,128]{2,1,0:T(8,128)} %get-tuple-element.9), calls=%async_computation.1 | async-start | bytes 393216 | tf_op jit(solution)/shard_map/all_to_all | solution.py:213
  25.5 0.6 slice_bitcast_fusion.refs_7_
  26.1 5.5 %all-to-all-done.1.refs_4_ = f32[8,48,128]{2,1,0:T(8,128)S(1)} async-done(((f32[8,48,128]{2,1,0:T(8,128)}), f32[8,48,128]{2,1,0:T(8,128)S(1)}, u32[]{:S(2)}, u32[]{:S(2)}) %all-to-all-start.1) | async-done | bytes 196640 | tf_op jit(solution)/shard_map/all_to_all | solution.py:213
  31.7 0.7 copy-done.5
  32.4 4.7 %shard_map.96 = (f32[16,64,48]{2,1,0:T(8,128)}, f32[8,48,128]{2,1,0:T(8,128)}) custom-call(s32[16]{0:T(128)} %cnt_ref.1, s32[16,8]{1,0:T(8,128)} %copy.41.refs_1_.col_ref, s32[16]{0:T(128)} %reshape.132.refs_2_.out_idx_ref, f32[16,64,48]{2,1,0:T(8,128)} %get-tuple-element.8.refs_3_, f32[8,48,128]{2,1,0:T(8,128)} %copy-done.5, f32[16,64,512]{2,1,0:T(8,128)} %refs_5_.3, ...), custom_call_target="tpu_custom_call" | custom-call | tf_op jit(solution)/shard_map/pallas_call | solution.py:224
  37.0 5.3 %shard_map.97 = (f32[16,64,48]{2,1,0:T(8,128)}, f32[8,96,128]{2,1,0:T(8,128)}) custom-call(s32[16]{0:T(128)} %cnt_ref.1, s32[16,8]{1,0:T(8,128)} %copy.41.refs_1_.col_ref, s32[16]{0:T(128)} %reshape.132.refs_2_.out_idx_ref, f32[16,64,48]{2,1,0:T(8,128)} %get-tuple-element.10.refs_3_.value_ref, f32[16,64,48]{2,1,0:T(8,128)} %bitcast.22, ...), custom_call_target="tpu_custom_call" | custom-call | tf_op jit(solution)/shard_map/pallas_call | solution.py:225
  42.3 3.5 %all-to-all-start.2 = ((f32[8,96,128]{2,1,0:T(8,128)}), f32[8,96,128]{2,1,0:T(8,128)S(1)}, u32[]{:S(2)}, u32[]{:S(2)}) async-start(f32[8,96,128]{2,1,0:T(8,128)} %get-tuple-element.13), calls=%async_computation.2 | async-start | bytes 786432 | tf_op jit(solution)/shard_map/all_to_all | solution.py:213
  45.8 0.7 gather_fusion
  46.5 0.6 pad_add_fusion.place_ref
  47.1 6.9 %all-to-all-done.2.returned_ref = f32[8,96,128]{2,1,0:T(8,128)S(1)} async-done(((f32[8,96,128]{2,1,0:T(8,128)}), f32[8,96,128]{2,1,0:T(8,128)S(1)}, u32[]{:S(2)}, u32[]{:S(2)}) %all-to-all-start.2) | async-done | bytes 393248 | tf_op jit(solution)/shard_map/all_to_all | solution.py:213
  54.0 0.7 copy-done.3
  54.8 6.5 %shard_map.98 = f32[8,16,2,64]{3,2,1,0:T(2,128)} custom-call(s32[16]{0:T(128)} %cnt_ref.1, s32[16,8]{1,0:T(8,128)} %copy.41.refs_1_.col_ref, s32[16]{0:T(128)} %reshape.132.refs_2_.out_idx_ref, s32[17]{0:T(128)} %pad_add_fusion.place_ref, f32[16,64,48]{2,1,0:T(8,128)} %get-tuple-element.10.refs_3_.value_ref, f32[16,64,48]{2,1,0:T(8,128)} %bitcast.24, ...), custom_call_target="tpu_custom_call" | custom-call | tf_op jit(solution)/shard_map/pallas_call | solution.py:238
  61.3 1.0 %reshape.167 = f32[32,1,512]{2,1,0:T(1,128)S(1)} reshape(f32[32,4,2,64]{3,2,1,0:T(2,128)} %bitcast.30) | data formatting | bytes 131072
  62.3 11.3 %all_to_all.20 = f32[32,1,512]{2,1,0:T(1,128)S(1)} all-to-all(f32[32,1,512]{2,1,0:T(1,128)S(1)} %reshape.167), channel_id=1, replica_groups=mesh['dom'=8,'dest'=4] {'dom','dest'}, dimensions={0} | all-to-all | bytes 131072 | tf_op jit(solution)/shard_map/all_to_all | solution.py:241
  73.6 0.5 broadcast.174
  74.1 0.8 %reduce.8 = f32[32,512]{1,0:T(8,128)S(1)} reduce(f32[32,1,512]{2,1,0:T(1,128)S(1)} %all_to_all.20, f32[]{:T(128)} %broadcast.174), dimensions={1}, to_apply=%all_to_all.15.reduce_sub_computation | reduce | bytes 131076 | tf_op jit(solution)/shard_map/all_to_all | solution.py:241
  75.2 0.6 reshape_squeeze.4
  75.8 0.6 neg.12
  (30 shorter events, 1.0 us)
Async XLA Ops:
  0.6 0.7 copy-start
  0.6 10.9 %copy-start.6 = (f32[48,1024]{1,0:T(8,128)S(1)}, f32[48,1024]{1,0:T(8,128)}, u32[]{:S(2)}) copy-start(f32[48,1024]{1,0:T(8,128)} %param.10) | copy-start | bytes 589828
  0.7 10.2 %copy-start.8 = (s32[16,8]{0,1:T(8,128)S(1)}, s32[16,8]{0,1:T(8,128)}, u32[]{:S(2)}) copy-start(s32[16,8]{0,1:T(8,128)} %param.14) | copy-start | bytes 1540
  0.7 11.9 %copy-start.7 = (f32[48,1024]{1,0:T(8,128)S(1)}, f32[48,1024]{1,0:T(8,128)}, u32[]{:S(2)}) copy-start(f32[48,1024]{1,0:T(8,128)} %param.11) | copy-start | bytes 589828
  0.7 12.1 %copy-start.1 = (f32[16,64,512]{2,1,0:T(8,128)S(1)}, f32[16,64,512]{2,1,0:T(8,128)}, u32[]{:S(2)}) copy-start(f32[16,64,512]{2,1,0:T(8,128)} %refs_5_.3) | copy-start | bytes 6291460
  5.0 11.4 %all-to-all-start = ((f32[8,48,128]{2,1,0:T(8,128)}), f32[8,48,128]{2,1,0:T(8,128)S(1)}, u32[]{:S(2)}, u32[]{:S(2)}) async-start(f32[8,48,128]{2,1,0:T(8,128)} %bitcast.18), calls=%async_computation | async-start | bytes 393216 | tf_op jit(solution)/shard_map/all_to_all | solution.py:213
  12.8 12.8 %copy-start.2 = (f32[48,1024]{0,1:T(8,128)}, f32[48,1024]{0,1:T(8,128)S(1)}, u32[]{:S(2)}) copy-start(f32[48,1024]{0,1:T(8,128)S(1)} %copy.38) | copy-start | bytes 589828
  16.4 1.0 %copy-start.4 = (f32[8,48,128]{2,1,0:T(8,128)}, f32[8,48,128]{2,1,0:T(8,128)S(1)}, u32[]{:S(2)}) copy-start(f32[8,48,128]{2,1,0:T(8,128)S(1)} %all-to-all-done.refs_4_) | copy-start | bytes 589828
  22.1 9.5 %all-to-all-start.1 = ((f32[8,48,128]{2,1,0:T(8,128)}), f32[8,48,128]{2,1,0:T(8,128)S(1)}, u32[]{:S(2)}, u32[]{:S(2)}) async-start(f32[8,48,128]{2,1,0:T(8,128)} %get-tuple-element.9), calls=%async_computation.1 | async-start | bytes 393216 | tf_op jit(solution)/shard_map/all_to_all | solution.py:213
  31.7 0.7 copy-start.5
  42.3 11.7 %all-to-all-start.2 = ((f32[8,96,128]{2,1,0:T(8,128)}), f32[8,96,128]{2,1,0:T(8,128)S(1)}, u32[]{:S(2)}, u32[]{:S(2)}) async-start(f32[8,96,128]{2,1,0:T(8,128)} %get-tuple-element.13), calls=%async_computation.2 | async-start | bytes 786432 | tf_op jit(solution)/shard_map/all_to_all | solution.py:213
  54.0 0.7 copy-start.3

commit v7 on v6

--- a/solution.py
+++ b/solution.py
@@ -146,6 +146,14 @@
             routed_out[p, blk, 1:2, :] = routed_out[p, blk, 1:2, :] + dest_sum(weight * product)
 
 
+def middle_kernel(cnt_ref, col_ref, out_idx_ref, value_ref, recv_ref, turn_ref, scale_ref, exit_ref,
+                  demand_ref, turn_t_ref, value_out, own_out, ghost_out, send, table, ratio, totals):
+    forward_kernel(True, cnt_ref, col_ref, out_idx_ref, value_ref, recv_ref, turn_ref, scale_ref,
+                   exit_ref, value_out, send, table)
+    adjoint_kernel(True, cnt_ref, col_ref, out_idx_ref, value_out, demand_ref, scale_ref, demand_ref,
+                   demand_ref, turn_t_ref, send, own_out, ghost_out, ratio, totals)
+
+
 def final_kernel(out_idx_ref, value_ref, demand_ref, scale_ref, own_ref, returned_ref, weight_ref,
                  flow_out, grad_out, owned):
     owned[...] = own_ref[...]
@@ -221,8 +229,18 @@
     )
     value, send = forward(True)(*idx, exit_t, received, turn_weight, scale, exit_t)
     received = exchange(send)
-    value, send = forward(True)(*idx, value, received, turn_weight, scale, exit_t)
-    own, ghost = adjoint(True)(*idx, value, demand_t, scale, demand_t, demand_t[:1], turn_t, send)
+    middle = pl.pallas_call(
+        middle_kernel,
+        out_shape=(
+            jax.ShapeDtypeStruct(block_shape, f32),
+            jax.ShapeDtypeStruct(block_shape, f32),
+            jax.ShapeDtypeStruct((partitions, 2 * columns, capacity * block_len), f32),
+        ),
+        in_specs=[smem, smem, smem] + [vmem] * 7,
+        out_specs=(vmem, vmem, vmem),
+        scratch_shapes=[pltpu.VMEM(ghost_shape, f32), scratch, pltpu.VMEM(block_shape, f32), scratch],
+    )
+    value, own, ghost = middle(*idx, value, received, turn_weight, scale, exit_t, demand_t, turn_t)
     returned = exchange(ghost)
     weight = dest_weight.reshape(1, columns)
     ghost_part = jnp.arange(ghosts, dtype=jnp.int32) // capacity

time: 77 us -> 75.1 us (0.975)
  Pallas kernels: 21.1 us -> 19.2 us
    pallas_call x2 -> x1, Pallas kernels: 9.95 us -> 8.04 us  [local(): middle(*idx, value, received, turn_weight, scale, exit_t, demand_t, turn_t)]
    transpose x0 -> x1, local copies, waits for them, and re-layouts: none -> 1.01 us  [local(): demand_t = demand.T.reshape(block_shape)]
    unnamed x23 -> x20, local copies, waits for them, and re-layouts: 6.85 us -> 6.66 us
  transfers between devices with their start and end apart: 3 -> 3, of which waited for: 3 -> 3; matrix products, arithmetic and copies ran while one was open for 9% -> 10% of each run, Pallas kernels for 0% -> 0%
where the time goes in v7:
time: 75.1 us; the launch traced here: 74.6 us
  Pallas kernels  19.2 us (26%)
  local copies, waits for them, and re-layouts  14.8 us (20%)
  waiting for transfers between devices  13.2 us (18%)
  starting transfers between devices  12.2 us (16%)
  blocking collectives  11.3 us (15%)
  other arithmetic  3.21 us (4%)
  between operations  0.77 us (1%)
    all_to_all x3, waiting for transfers between devices, exchange(): lax.all_to_all(pieces, 'dom', split_axis=0, concat_axis=0, tiled=True)  13.2 us
    all_to_all x3, starting transfers between devices, exchange(): lax.all_to_all(pieces, 'dom', split_axis=0, concat_axis=0, tiled=True)  12.2 us
    all_to_all x1, blocking collectives, local(): lax.all_to_all(routed, ('dom', 'dest'), split_axis=0, concat_axis=0, tile...  11.3 us
    pallas_call x1, Pallas kernels, local(): middle(*idx, value, received, turn_weight, scale, exit_t, demand_t, turn_t)  8.04 us
    unnamed x20, local copies, waits for them, and re-layouts  6.66 us
    pallas_call x1, Pallas kernels, local(): last(*idx, place, value, demand_t, scale, own, returned, turn_t, weight)  6.51 us
    pallas_call x1, Pallas kernels, local(): forward(True)(*idx, exit_t, received, turn_weight, scale, exit_t)  4.67 us
  transfers between devices with their start and end apart: 3, of which 3 were waited for; matrix products, arithmetic and copies ran while one was open for 10% of the time, Pallas kernels for 0%

profile of v7, /device:TPU:0, one launch (start us, length us, event | category | flops | bytes accessed | tf_op | source)
XLA Modules:
  0.0 74.6 jit_solution(13531181107130044141)
XLA Ops:
  0.7 0.7 copy-done
  1.4 0.7 negate_exponential_fusion
  2.1 0.9 %broadcast_multiply_fusion = f32[48,1024]{1,0:T(8,128)S(1)} fusion(f32[48,1024]{1,0:T(8,128)} %param.10, f32[1024]{0:T(1024)S(1)} %negate_exponential_fusion), kind=kLoop, calls=%fused_computation.3 | loop fusion | flops 49152 | bytes 397312 | tf_op jit(solution)/shard_map/mul | solution.py:226
  3.2 0.1 copy.31
  3.4 0.6 gather_fusion.1
  4.0 0.1 copy.32
  4.3 0.7 copy.40
  5.0 5.2 %all-to-all-start = ((f32[8,48,128]{2,1,0:T(8,128)}), f32[8,48,128]{2,1,0:T(8,128)S(1)}, u32[]{:S(2)}, u32[]{:S(2)}) async-start(f32[8,48,128]{2,1,0:T(8,128)} %bitcast.15), calls=%async_computation | async-start | bytes 393216 | tf_op jit(solution)/shard_map/all_to_all | solution.py:221
  10.2 0.6 reshape.131.refs_2_.out_idx_ref
  10.8 0.7 copy.38.refs_1_.col_ref
  11.5 1.0 %copy.29 = f32[1024,48]{1,0:T(8,128)} copy(f32[1024,48]{0,1:T(8,128)S(1)} %bitcast.24) | data formatting | bytes 393216 | tf_op jit(solution)/shard_map/transpose | solution.py:223
  12.5 3.9 %all-to-all-done.refs_4_ = f32[8,48,128]{2,1,0:T(8,128)S(1)} async-done(((f32[8,48,128]{2,1,0:T(8,128)}), f32[8,48,128]{2,1,0:T(8,128)S(1)}, u32[]{:S(2)}, u32[]{:S(2)}) %all-to-all-start) | async-done | bytes 196640 | tf_op jit(solution)/shard_map/all_to_all | solution.py:221
  16.4 1.0 %broadcast_in_dim.16.refs_6_.scale_ref = f32[16,64,48]{2,1,0:T(8,128)} broadcast(f32[16,64]{1,0:T(8,128)S(1)} %broadcast_in_dim.7), dimensions={0,1} | broadcast | bytes 200704 | tf_op jit(solution)/shard_map/broadcast_in_dim | solution.py:181
  17.4 4.7 %shard_map.95 = (f32[16,64,48]{2,1,0:T(8,128)}, f32[8,48,128]{2,1,0:T(8,128)}) custom-call(s32[16]{0:T(128)} %cnt_ref.3, s32[16,8]{1,0:T(8,128)} %copy.38.refs_1_.col_ref, s32[16]{0:T(128)} %reshape.131.refs_2_.out_idx_ref, f32[16,64,48]{2,1,0:T(8,128)} %bitcast.18, f32[8,48,128]{2,1,0:T(8,128)} %copy-done.3, f32[16,64,512]{2,1,0:T(8,128)} %turn_ref.1, ...), custom_call_target="tpu_custom_call" | custom-call | tf_op jit(solution)/shard_map/pallas_call | solution.py:230
  22.1 3.5 %all-to-all-start.1 = ((f32[8,48,128]{2,1,0:T(8,128)}), f32[8,48,128]{2,1,0:T(8,128)S(1)}, u32[]{:S(2)}, u32[]{:S(2)}) async-start(f32[8,48,128]{2,1,0:T(8,128)} %get-tuple-element.8), calls=%async_computation.1 | async-start | bytes 393216 | tf_op jit(solution)/shard_map/all_to_all | solution.py:221
  25.6 2.7 %copy.36 = f32[16,64,512]{1,2,0:T(8,128)} copy(f32[16,64,512]{2,1,0:T(8,128)S(1)} %copy-done.1) | data formatting | bytes 4194304 | tf_op args[1]
  28.3 1.0 %copy.35 = f32[1024,48]{1,0:T(8,128)} copy(f32[1024,48]{0,1:T(8,128)S(1)} %bitcast.26) | data formatting | bytes 393216 | tf_op jit(solution)/shard_map/transpose | solution.py:224
  29.3 2.4 %all-to-all-done.1.recv_ref = f32[8,48,128]{2,1,0:T(8,128)S(1)} async-done(((f32[8,48,128]{2,1,0:T(8,128)}), f32[8,48,128]{2,1,0:T(8,128)S(1)}, u32[]{:S(2)}, u32[]{:S(2)}) %all-to-all-start.1) | async-done | bytes 196640 | tf_op jit(solution)/shard_map/all_to_all | solution.py:221
  31.7 0.7 copy-done.5
  32.4 8.0 %shard_map.96 = (f32[16,64,48]{2,1,0:T(8,128)}, f32[16,64,48]{2,1,0:T(8,128)}, f32[8,96,128]{2,1,0:T(8,128)}) custom-call(s32[16]{0:T(128)} %cnt_ref.3, s32[16,8]{1,0:T(8,128)} %copy.38.refs_1_.col_ref, s32[16]{0:T(128)} %reshape.131.refs_2_.out_idx_ref, f32[16,64,48]{2,1,0:T(8,128)} %get-tuple-element.7.value_ref, f32[8,48,128]{2,1,0:T(8,128)} %copy-done.5, ...), custom_call_target="tpu_custom_call" | custom-call | tf_op jit(solution)/shard_map/pallas_call | solution.py:243
  40.4 3.5 %all-to-all-start.2 = ((f32[8,96,128]{2,1,0:T(8,128)}), f32[8,96,128]{2,1,0:T(8,128)S(1)}, u32[]{:S(2)}, u32[]{:S(2)}) async-start(f32[8,96,128]{2,1,0:T(8,128)} %get-tuple-element.11), calls=%async_computation.2 | async-start | bytes 786432 | tf_op jit(solution)/shard_map/all_to_all | solution.py:221
  43.9 0.7 gather_fusion
  44.6 0.6 pad_add_fusion.place_ref
  45.2 6.9 %all-to-all-done.2.returned_ref = f32[8,96,128]{2,1,0:T(8,128)S(1)} async-done(((f32[8,96,128]{2,1,0:T(8,128)}), f32[8,96,128]{2,1,0:T(8,128)S(1)}, u32[]{:S(2)}, u32[]{:S(2)}) %all-to-all-start.2) | async-done | bytes 393248 | tf_op jit(solution)/shard_map/all_to_all | solution.py:221
  52.1 0.8 %copy-done.2 = f32[8,96,128]{2,1,0:T(8,128)} copy-done((f32[8,96,128]{2,1,0:T(8,128)}, f32[8,96,128]{2,1,0:T(8,128)S(1)}, u32[]{:S(2)}) %copy-start.2) | copy-done | bytes 393240
  52.9 6.5 %shard_map.97 = f32[8,16,2,64]{3,2,1,0:T(2,128)} custom-call(s32[16]{0:T(128)} %cnt_ref.3, s32[16,8]{1,0:T(8,128)} %copy.38.refs_1_.col_ref, s32[16]{0:T(128)} %reshape.131.refs_2_.out_idx_ref, s32[17]{0:T(128)} %pad_add_fusion.place_ref, f32[16,64,48]{2,1,0:T(8,128)} %get-tuple-element.9.value_ref, f32[16,64,48]{2,1,0:T(8,128)} %bitcast.22, ...), custom_call_target="tpu_custom_call" | custom-call | tf_op jit(solution)/shard_map/pallas_call | solution.py:256
  59.4 1.0 %reshape.166 = f32[32,1,512]{2,1,0:T(1,128)S(1)} reshape(f32[32,4,2,64]{3,2,1,0:T(2,128)} %bitcast.25) | data formatting | bytes 131072
  60.5 11.3 %all_to_all.20 = f32[32,1,512]{2,1,0:T(1,128)S(1)} all-to-all(f32[32,1,512]{2,1,0:T(1,128)S(1)} %reshape.166), channel_id=1, replica_groups=mesh['dom'=8,'dest'=4] {'dom','dest'}, dimensions={0} | all-to-all | bytes 131072 | tf_op jit(solution)/shard_map/all_to_all | solution.py:259
  71.7 0.5 broadcast.174
  72.2 0.8 %reduce.8 = f32[32,512]{1,0:T(8,128)S(1)} reduce(f32[32,1,512]{2,1,0:T(1,128)S(1)} %all_to_all.20, f32[]{:T(128)} %broadcast.174), dimensions={1}, to_apply=%all_to_all.15.reduce_sub_computation | reduce | bytes 131076 | tf_op jit(solution)/shard_map/all_to_all | solution.py:259
  73.3 0.6 reshape_squeeze.4
  73.9 0.6 neg.12
  (26 shorter events, 0.8 us)
Async XLA Ops:
  0.6 0.7 copy-start
  0.6 10.9 %copy-start.4 = (f32[48,1024]{1,0:T(8,128)S(1)}, f32[48,1024]{1,0:T(8,128)}, u32[]{:S(2)}) copy-start(f32[48,1024]{1,0:T(8,128)} %param.10) | copy-start | bytes 589828
  0.7 10.2 %copy-start.7 = (s32[16,8]{0,1:T(8,128)S(1)}, s32[16,8]{0,1:T(8,128)}, u32[]{:S(2)}) copy-start(s32[16,8]{0,1:T(8,128)} %param.14) | copy-start | bytes 1540
  3.4 22.2 %copy-start.1 = (f32[16,64,512]{2,1,0:T(8,128)S(1)}, f32[16,64,512]{2,1,0:T(8,128)}, u32[]{:S(2)}) copy-start(f32[16,64,512]{2,1,0:T(8,128)} %turn_ref.1) | copy-start | bytes 6291460
  5.0 11.4 %all-to-all-start = ((f32[8,48,128]{2,1,0:T(8,128)}), f32[8,48,128]{2,1,0:T(8,128)S(1)}, u32[]{:S(2)}, u32[]{:S(2)}) async-start(f32[8,48,128]{2,1,0:T(8,128)} %bitcast.15), calls=%async_computation | async-start | bytes 393216 | tf_op jit(solution)/shard_map/all_to_all | solution.py:221
  16.4 1.0 %copy-start.3 = (f32[8,48,128]{2,1,0:T(8,128)}, f32[8,48,128]{2,1,0:T(8,128)S(1)}, u32[]{:S(2)}) copy-start(f32[8,48,128]{2,1,0:T(8,128)S(1)} %all-to-all-done.refs_4_) | copy-start | bytes 589828
  22.1 6.2 %copy-start.6 = (f32[48,1024]{1,0:T(8,128)S(1)}, f32[48,1024]{1,0:T(8,128)}, u32[]{:S(2)}) copy-start(f32[48,1024]{1,0:T(8,128)} %param.11) | copy-start | bytes 589828
  22.1 9.7 %all-to-all-start.1 = ((f32[8,48,128]{2,1,0:T(8,128)}), f32[8,48,128]{2,1,0:T(8,128)S(1)}, u32[]{:S(2)}, u32[]{:S(2)}) async-start(f32[8,48,128]{2,1,0:T(8,128)} %get-tuple-element.8), calls=%async_computation.1 | async-start | bytes 393216 | tf_op jit(solution)/shard_map/all_to_all | solution.py:221
  31.7 0.7 copy-start.5
  40.4 11.7 %all-to-all-start.2 = ((f32[8,96,128]{2,1,0:T(8,128)}), f32[8,96,128]{2,1,0:T(8,128)S(1)}, u32[]{:S(2)}, u32[]{:S(2)}) async-start(f32[8,96,128]{2,1,0:T(8,128)} %get-tuple-element.11), calls=%async_computation.2 | async-start | bytes 786432 | tf_op jit(solution)/shard_map/all_to_all | solution.py:221
  52.1 0.8 %copy-start.2 = (f32[8,96,128]{2,1,0:T(8,128)}, f32[8,96,128]{2,1,0:T(8,128)S(1)}, u32[]{:S(2)}) copy-start(f32[8,96,128]{2,1,0:T(8,128)S(1)} %all-to-all-done.2.returned_ref) | copy-start | bytes 1179652
